TPU v7x, 512 devices: a whole 4x4x16 slice. The times are simulated.
512 devices in a mesh: ctx: 32 (over z, core), head: 16 (over x, y).
Axes of the slice: x: 4, y: 4, z: 16, core: 2. Of those that a mesh axis runs over, the one named last changes fastest.
Arguments:
- attn_q: bfloat16 [4096, 4096], P('ctx', 'head'), may hold values from -6 to 6
- attn_k: bfloat16 [4096, 512], P('ctx'), may hold values from -6 to 6
- attn_v: bfloat16 [4096, 512], P('ctx'), may hold values from -0.375 to 0.375
- attn_cot: bfloat16 [4096, 4096], P('ctx', 'head'), may hold values from -6 to 6
- attn_lse: float32 [16, 4096], P('head'), may hold values from 3 to 6
- attn_delta: float32 [16, 4096], P('head'), may hold values from -6 to 6
- block_lists: int32 [16, 64, 4], P('head'), may hold values from 0 to 63, as said below
- gdn_q: bfloat16 [4096, 2048], P('ctx', 'head'), may hold values from -6 to 6
- gdn_k: bfloat16 [4096, 2048], P('ctx', 'head'), may hold values from -6 to 6
- gdn_v: bfloat16 [4096, 4096], P('ctx', 'head'), may hold values from -6 to 6
- decay_logit: float32 [32, 4096], P('head', 'ctx'), may hold values from -8 to 8
- write_logit: float32 [32, 4096], P('head', 'ctx'), may hold values from -6 to 6
- decay_rate: float32 [32], P('head'), may hold values from 0.00024414062 to 0.1
- write_scale: float32 [32], P('head'), may hold values from 0.05 to 1
- gdn_cot: bfloat16 [4096, 4096], P('ctx', 'head'), may hold values from -6 to 6
Outputs:
- attn_dq: float32 [4096, 4096], P('ctx', 'head')
- attn_dk: float32 [4096, 512], P('ctx')
- attn_dv: float32 [4096, 512], P('ctx')
- gdn_dq: float32 [4096, 2048], P('ctx', 'head')
- gdn_dk: float32 [4096, 2048], P('ctx', 'head')
- gdn_dv: float32 [4096, 4096], P('ctx', 'head')
- gdn_ddecay: float32 [32, 4096], P('head', 'ctx')
- gdn_dwrite: float32 [32, 4096], P('head', 'ctx')
Inputs may be any that keep to these rules, and one draw needn't show every extreme that they name: `block_lists`: entries for query block b lie in 0 to b and may repeat.
All inputs are finite; a program needn't handle non-finite values.
Results may differ from a plain program's by a relative error of at most 0.00035.
Values may be sent and summed in bfloat16 or wider, within the bound.
No kernel may reach another device: no remote copies, remote signals or barrier semaphores. Data moves between devices by JAX's collectives and lax.ppermute only.
A program may use at most 128 MiB of HBM per device.

v0:
```python
import jax
import jax.numpy as jnp
from jax import lax
from jax.sharding import PartitionSpec as P

Q_HEADS = 16
KV_HEADS = 2
HD = 256
GDIM = 128
BLK = 64
TOPK = 4
SPAN = 64


HIGHEST = lax.Precision.HIGHEST


def prefix(value, axis, join, neutral, backward):
    count, mine = (lax.axis_size(axis), lax.axis_index(axis))
    pieces = jax.tree.map(lambda part: lax.all_gather(part, axis), value)
    if backward:
        pieces = jax.tree.map(lambda part: part[::-1], pieces)
        mine = count - 1 - mine
    so_far = jax.tree.map(
        lambda part, zero: jnp.full_like(part, 0) + jnp.asarray(zero, part.dtype), value, neutral
    )

    def turn(position, so_far):
        longer = join(so_far, jax.tree.map(lambda part: part[position], pieces))
        return jax.tree.map(lambda new, old: jnp.where(position < mine, new, old), longer, so_far)

    return lax.fori_loop(0, count - 1, turn, so_far)


def unit_rows(matrix):
    return matrix / jnp.sqrt(jnp.sum(matrix * matrix, axis=-1, keepdims=True) + 1e-06)


def span_update(memory, packed):
    queries, keys_in, values_in, log_decay, write_gain = packed
    length = log_decay.shape[-1]
    cum_log = jnp.cumsum(log_decay, axis=-1)
    log_gap = cum_log[:, :, None] - cum_log[:, None, :]
    order_ids = jnp.arange(length)
    strict_low = order_ids[:, None] > order_ids[None, :]
    with_diag = order_ids[:, None] >= order_ids[None, :]
    decay_strict = jnp.where(strict_low, jnp.exp(jnp.where(strict_low, log_gap, 0.0)), 0.0)
    decay_upto = jnp.where(with_diag, jnp.exp(jnp.where(with_diag, log_gap, 0.0)), 0.0)
    key_gram = jnp.einsum("htd,hsd->hts", keys_in, keys_in, precision=HIGHEST)
    system = write_gain[:, :, None] * decay_strict * key_gram + jnp.eye(length, dtype=jnp.float32)
    decay_now = jnp.exp(cum_log)
    recalled = jnp.einsum("hvd,htd->htv", memory, keys_in, precision=HIGHEST)
    target = write_gain[:, :, None] * (values_in - decay_now[:, :, None] * recalled)
    written = lax.linalg.triangular_solve(
        system, target, left_side=True, lower=True, unit_diagonal=True
    )
    read_old = jnp.einsum("hvd,htd->htv", memory, queries, precision=HIGHEST)
    query_key = jnp.einsum("htd,hsd->hts", queries, keys_in, precision=HIGHEST)
    outputs = decay_now[:, :, None] * read_old + jnp.einsum(
        "hts,hsv->htv", decay_upto * query_key, written, precision=HIGHEST
    )
    tail_decay = jnp.exp(cum_log[:, -1:] - cum_log)
    memory_next = jnp.exp(cum_log[:, -1])[:, None, None] * memory + jnp.einsum(
        "hsv,hsd->hvd", written * tail_decay[:, :, None], keys_in, precision=HIGHEST
    )
    return (memory_next, outputs)


def delta_forward(raw_inputs, memory, rate_heads, scale_heads):
    query_raw, key_raw, value_raw, decay_in, write_in = raw_inputs
    n_tokens = query_raw.shape[0]
    key_heads = query_raw.shape[1] // GDIM
    value_heads = value_raw.shape[1] // GDIM
    ratio_heads = value_heads // key_heads
    n_spans = n_tokens // SPAN
    queries = jnp.repeat(
        unit_rows(query_raw.reshape(n_tokens, key_heads, GDIM)), ratio_heads, axis=1
    )
    keys_norm = jnp.repeat(
        unit_rows(key_raw.reshape(n_tokens, key_heads, GDIM)), ratio_heads, axis=1
    )
    values_in = value_raw.reshape(n_tokens, value_heads, GDIM)
    log_decay = -rate_heads[:, None] * jax.nn.softplus(decay_in)
    write_gain = scale_heads[:, None] * jax.nn.sigmoid(write_in)

    def blocks_of(tensor):
        return tensor.reshape(n_spans, SPAN, value_heads, GDIM).transpose(0, 2, 1, 3)

    def gates_of(tensor):
        return tensor.reshape(value_heads, n_spans, SPAN).transpose(1, 0, 2)

    memory_end, outputs = lax.scan(
        span_update,
        memory,
        (
            blocks_of(queries),
            blocks_of(keys_norm),
            blocks_of(values_in),
            gates_of(log_decay),
            gates_of(write_gain),
        ),
    )
    return (outputs.transpose(0, 2, 1, 3).reshape(n_tokens, value_heads * GDIM), memory_end)


def sparse_query_grad(
    q_blocks,
    cot_blocks,
    own_keys,
    own_values,
    listed_keys,
    listed_values,
    lse_rows,
    delta_rows,
    head_lists,
    block_ids,
):
    score_scale = HD ** (-0.5)
    position = jnp.arange(BLK)
    causal = position[:, None] >= position[None, :]
    slot_ids = jnp.arange(TOPK)
    repeated = jnp.any(
        (head_lists[:, :, None] == head_lists[:, None, :])
        & (slot_ids[:, None] > slot_ids[None, :]),
        axis=2,
    )
    usable = (head_lists < block_ids[:, None]) & jnp.logical_not(repeated)
    own_score = (
        jnp.einsum("bid,bjd->bij", q_blocks, own_keys, preferred_element_type=jnp.float32)
        * score_scale
    )
    list_score = (
        jnp.einsum("bid,btjd->bitj", q_blocks, listed_keys, preferred_element_type=jnp.float32)
        * score_scale
    )
    own_prob = jnp.where(causal[None], jnp.exp(own_score - lse_rows[:, :, None]), 0.0)
    list_prob = jnp.where(
        usable[:, None, :, None], jnp.exp(list_score - lse_rows[:, :, None, None]), 0.0
    )
    own_dprob = jnp.einsum(
        "bid,bjd->bij", cot_blocks, own_values, preferred_element_type=jnp.float32
    )
    list_dprob = jnp.einsum(
        "bid,btjd->bitj", cot_blocks, listed_values, preferred_element_type=jnp.float32
    )
    own_dscore = own_prob * (own_dprob - delta_rows[:, :, None])
    list_dscore = list_prob * (list_dprob - delta_rows[:, :, None, None])
    own_part = jnp.einsum(
        "bij,bjd->bid", own_dscore, own_keys.astype(jnp.float32), precision=HIGHEST
    )
    list_part = jnp.einsum(
        "bitj,btjd->bid", list_dscore, listed_keys.astype(jnp.float32), precision=HIGHEST
    )
    return (own_part + list_part) * score_scale


def compose_maps(earlier, later):
    product = jnp.einsum("hij,hjk->hik", earlier[0], later[0], precision=HIGHEST)
    shifted = jnp.einsum("hij,hjk->hik", earlier[1], later[0], precision=HIGHEST) + later[1]
    return (product, shifted)


def on_device(
    attn_q,
    attn_k,
    attn_v,
    attn_cot,
    attn_lse,
    attn_delta,
    block_lists,
    gdn_q,
    gdn_k,
    gdn_v,
    decay_logit,
    write_logit,
    decay_rate,
    write_scale,
    gdn_cot,
):
    score_scale = HD ** (-0.5)
    head_index = lax.axis_index("head")
    ctx_index = lax.axis_index("ctx")
    tok_rows = attn_q.shape[0]
    local_heads = attn_q.shape[1] // HD
    blocks_here = tok_rows // BLK
    kv_group = head_index * local_heads // (Q_HEADS // KV_HEADS)
    own_keys = lax.dynamic_index_in_dim(
        attn_k.reshape(tok_rows, KV_HEADS, HD), kv_group, 1, keepdims=False
    )
    own_values = lax.dynamic_index_in_dim(
        attn_v.reshape(tok_rows, KV_HEADS, HD), kv_group, 1, keepdims=False
    )
    row_base = ctx_index * tok_rows
    first_block = ctx_index * blocks_here
    key_block_ids = first_block + jnp.arange(blocks_here, dtype=jnp.int32)
    member = jnp.any(block_lists[:, :, :, None] == key_block_ids[None, None, None, :], axis=2)
    member_rows = jnp.repeat(jnp.repeat(member, BLK, axis=1), BLK, axis=2)
    key_pos = row_base + jnp.arange(tok_rows, dtype=jnp.int32)
    key_block = key_pos // BLK
    keys_whole, values_whole = (
        lax.all_gather(own_keys, "ctx", axis=0, tiled=True),
        lax.all_gather(own_values, "ctx", axis=0, tiled=True),
    )
    lists_own = lax.dynamic_slice_in_dim(block_lists, first_block, blocks_here, 1)
    lse_own = lax.dynamic_slice_in_dim(attn_lse, row_base, tok_rows, 1).reshape(
        local_heads, blocks_here, BLK
    )
    delta_own = lax.dynamic_slice_in_dim(attn_delta, row_base, tok_rows, 1).reshape(
        local_heads, blocks_here, BLK
    )
    q_blocks = attn_q.reshape(blocks_here, BLK, local_heads, HD).transpose(2, 0, 1, 3)
    cot_blocks = attn_cot.reshape(blocks_here, BLK, local_heads, HD).transpose(2, 0, 1, 3)
    listed_keys = keys_whole.reshape(-1, BLK, HD)[lists_own]
    listed_values = values_whole.reshape(-1, BLK, HD)[lists_own]
    grad_blocks = jax.vmap(sparse_query_grad, in_axes=(0, 0, None, None, 0, 0, 0, 0, 0, None))(
        q_blocks,
        cot_blocks,
        own_keys.reshape(blocks_here, BLK, HD),
        own_values.reshape(blocks_here, BLK, HD),
        listed_keys,
        listed_values,
        lse_own,
        delta_own,
        lists_own,
        key_block_ids,
    )
    grad_q = grad_blocks.transpose(1, 2, 0, 3).reshape(tok_rows, local_heads * HD)
    query_rows = lax.all_gather(attn_q, "ctx", axis=0, tiled=True)
    n_rows = query_rows.shape[0]
    queries = query_rows.reshape(n_rows, local_heads, HD)
    cotangent = lax.all_gather(attn_cot, "ctx", axis=0, tiled=True).reshape(n_rows, local_heads, HD)
    row_pos = jnp.arange(n_rows, dtype=jnp.int32)
    row_block = row_pos // BLK
    own_pair = (row_block[:, None] == key_block[None, :]) & (row_pos[:, None] >= key_pos[None, :])
    listed_pair = member_rows & (key_block[None, :] < row_block[:, None])[None]
    allowed = own_pair[None] | listed_pair
    scores = (
        jnp.einsum("nhd,kd->hnk", queries, own_keys, preferred_element_type=jnp.float32)
        * score_scale
    )
    prob_full = jnp.where(allowed, jnp.exp(scores - attn_lse[:, :, None]), 0.0)
    dprobs = jnp.einsum("nhd,kd->hnk", cotangent, own_values, preferred_element_type=jnp.float32)
    dscores = prob_full * (dprobs - attn_delta[:, :, None])
    grad_value = jnp.einsum(
        "hnk,nhd->kd", prob_full, cotangent.astype(jnp.float32), precision=HIGHEST
    )
    grad_key = (
        jnp.einsum("hnk,nhd->kd", dscores, queries.astype(jnp.float32), precision=HIGHEST)
        * score_scale
    )
    slot_mask = (jnp.arange(KV_HEADS) == kv_group)[None, :, None]
    key_slots = jnp.where(slot_mask, grad_key[:, None, :], 0.0).reshape(tok_rows, KV_HEADS * HD)
    value_slots = jnp.where(slot_mask, grad_value[:, None, :], 0.0).reshape(tok_rows, KV_HEADS * HD)
    attn_dk, attn_dv = lax.psum((key_slots, value_slots), "head")
    raw_inputs = (
        gdn_q.astype(jnp.float32),
        gdn_k.astype(jnp.float32),
        gdn_v.astype(jnp.float32),
        decay_logit,
        write_logit,
    )
    value_heads = gdn_v.shape[1] // GDIM
    zero_memory = jnp.zeros((value_heads, GDIM, GDIM), jnp.float32)
    unit_memory = jnp.broadcast_to(jnp.eye(GDIM, dtype=jnp.float32), zero_memory.shape)

    def local_run(raw_values, memory):
        return delta_forward(raw_values, memory, decay_rate, write_scale)

    silent_inputs = (
        raw_inputs[0],
        raw_inputs[1],
        jnp.zeros_like(raw_inputs[2]),
        raw_inputs[3],
        raw_inputs[4],
    )
    transition = local_run(silent_inputs, unit_memory)[1]
    outputs_zero, pull_zero = jax.vjp(local_run, raw_inputs, zero_memory)
    written_end = outputs_zero[1]
    cot_full = gdn_cot.astype(jnp.float32)
    local_grad = pull_zero((cot_full, zero_memory))[1]
    memory_in = prefix(
        (transition, written_end), "ctx", compose_maps, (unit_memory, zero_memory), False
    )[1]
    flipped = jnp.swapaxes(transition, 1, 2)
    memory_grad = prefix(
        (flipped, local_grad), "ctx", compose_maps, (unit_memory, zero_memory), True
    )[1]
    unused_out, pull_final = jax.vjp(local_run, raw_inputs, memory_in)
    grads = pull_final((cot_full, memory_grad))[0]
    return (grad_q, attn_dk, attn_dv, grads[0], grads[1], grads[2], grads[3], grads[4])


def solution(mesh):
    return jax.shard_map(
        on_device,
        mesh=mesh,
        in_specs=(
            P("ctx", "head"),
            P("ctx", None),
            P("ctx", None),
            P("ctx", "head"),
            P("head", None),
            P("head", None),
            P("head", None, None),
            P("ctx", "head"),
            P("ctx", "head"),
            P("ctx", "head"),
            P("head", "ctx"),
            P("head", "ctx"),
            P("head"),
            P("head"),
            P("ctx", "head"),
        ),
        out_specs=(
            P("ctx", "head"),
            P("ctx", None),
            P("ctx", None),
            P("ctx", "head"),
            P("ctx", "head"),
            P("ctx", "head"),
            P("head", "ctx"),
            P("head", "ctx"),
        ),
        check_vma=False,
    )
```

profile of v0, /device:TPU:1, one launch (start us, length us, event | category | flops | bytes accessed | tf_op | source)
XLA Modules:
  0.0 767.3 jit_solution(10239268752019939677)
XLA Ops:
  20.4 24.4 %while.177 = (s32[]{:T(128)}, f32[2,128,128]{2,1,0:T(8,128)S(1)}, f32[2,2,64,1]{2,1,3,0:T(2,128)S(1)}, f32[2,2,64,1]{2,1,3,0:T(2,128)S(1)}, f32[2,2,64,64]{3,2,1...) while((s32[]{:T(128)}, f32[2,128,128]{2,1,0:T(8,128)S(1)}, ...), condition=%wide.region_11.13_spmd.clone.clone, body=%wide.region_9.12_spmd.clone.clone.sunk | while | flops 88404160 | bytes 1473784 | solution.py:92
  21.7 9.9 %custom-call.48 = f32[2,1,64,64]{2,3,1,0:T(8,128)S(1)} custom-call(f32[2,1,64,64]{3,2,1,0:T(8,128)S(1)} %add_bitcast_fusion.8), custom_call_target="InvertDiagBlocksLowerTriangular" | custom-call | tf_op jit(solution)/shard_map/jvp()/while/body/eval_jaxpr/triangular_solve/custom-call.1 | solution.py:54
  33.9 9.9 %custom-call.48 = f32[2,1,64,64]{2,3,1,0:T(8,128)S(1)} custom-call(f32[2,1,64,64]{3,2,1,0:T(8,128)S(1)} %add_bitcast_fusion.8), custom_call_target="InvertDiagBlocksLowerTriangular" | custom-call | tf_op jit(solution)/shard_map/jvp()/while/body/eval_jaxpr/triangular_solve/custom-call.1 | solution.py:54
  45.5 23.5 %while.174 = (s32[]{:T(128)}, f32[2,128,128]{2,1,0:T(8,128)S(1)}, f32[2,2,1,1]{1,3,2,0:T(1,128)S(1)}, f32[2,2,64,1]{2,1,3,0:T(2,128)S(1)}, f32[2,2,64,128]{3,2,1...) while((s32[]{:T(128)}, f32[2,128,128]{2,1,0:T(8,128)S(1)}, ...), condition=%wide.region_13.16_spmd.clone, body=%wide.region_12.15_spmd.clone.sunk | while | flops 100954176 | bytes 1590971 | solution.py:92
  46.3 9.8 %custom-call.47 = f32[2,1,64,64]{2,3,1,0:T(8,128)S(1)} custom-call(f32[2,1,64,64]{3,2,1,0:T(8,128)S(1)} %fusion.505), custom_call_target="InvertDiagBlocksLowerTriangular" | custom-call | tf_op jit(solution)/shard_map/transpose(jvp())/while/body/eval_jaxpr/triangular_solve/custom-call.0 | solution.py:54
  58.1 9.8 %custom-call.47 = f32[2,1,64,64]{2,3,1,0:T(8,128)S(1)} custom-call(f32[2,1,64,64]{3,2,1,0:T(8,128)S(1)} %fusion.505), custom_call_target="InvertDiagBlocksLowerTriangular" | custom-call | tf_op jit(solution)/shard_map/transpose(jvp())/while/body/eval_jaxpr/triangular_solve/custom-call.0 | solution.py:54
  69.9 23.7 %while.171 = (s32[]{:T(128)}, f32[2,128,128]{2,1,0:T(8,128)S(1)}, f32[2,2,64]{2,1,0:T(2,128)S(1)}, f32[2,2,64]{2,1,0:T(2,128)S(1)}, f32[2,2,64,128]{3,2,1,0:T(8,128)S(1)}, /*index=5*/s32[]{:T(128)}, f32[]{:T(128)}) while((s32[]{:T(128)}, f32[2,128,128]{2,1,0:T(8,128)S(1)}, f32[2,2,64]{2,1,0:T(2,128)S(1)}, f32[2,2,64]{2,1,0:T(2,128)S(1)}, ...), condition=%wide.region_7.9_spmd, body=%wide.region_5.8_spmd.sunk | while | flops 75726912 | bytes 1051785 | solution.py:92
  71.1 9.8 %custom-call.43 = f32[2,1,64,64]{2,3,1,0:T(8,128)S(1)} custom-call(f32[2,1,64,64]{3,2,1,0:T(8,128)S(1)} %fusion.440), custom_call_target="InvertDiagBlocksLowerTriangular" | custom-call | tf_op jit(solution)/shard_map/while/body/eval_jaxpr/triangular_solve/custom-call.1 | solution.py:54
  83.0 9.8 %custom-call.43 = f32[2,1,64,64]{2,3,1,0:T(8,128)S(1)} custom-call(f32[2,1,64,64]{3,2,1,0:T(8,128)S(1)} %fusion.440), custom_call_target="InvertDiagBlocksLowerTriangular" | custom-call | tf_op jit(solution)/shard_map/while/body/eval_jaxpr/triangular_solve/custom-call.1 | solution.py:54
  102.2 2.9 fusion.267
  105.0 53.9 %all-gather.17.cloned.1.call-done = bf16[4096,256]{1,0:T(8,128)(2,1)} async-done(((bf16[128,256]{1,0:T(8,128)(2,1)}), bf16[4096,256]{1,0:T(8,128)(2,1)}) %all-gather.17.cloned.1.call-update) | async-done | bytes 2097168 | tf_op jit(solution)/shard_map/all_gather | solution.py:231
  158.9 2.6 fusion.271
  161.5 1.3 convolution_multiply_fusion.11
  165.2 66.4 %all-gather.21.cloned.1.call-done = bf16[4096,1,256]{0,2,1:T(8,128)(2,1)} async-done(((bf16[128,1,256]{0,2,1:T(8,128)(2,1)}), bf16[4096,1,256]{0,2,1:T(8,128)(2,1)}) %all-gather.21.cloned.1.call-update) | async-done | bytes 2097168 | tf_op jit(solution)/shard_map/all_gather | solution.py:202
  231.6 3.3 copy.174
  234.9 1.4 gather_fusion.1
  236.3 65.2 %all-gather.19.cloned.1.call-done = bf16[4096,1,256]{2,0,1:T(8,128)(2,1)} async-done(((bf16[128,1,256]{2,0,1:T(8,128)(2,1)}), bf16[4096,1,256]{2,0,1:T(8,128)(2,1)}) %all-gather.19.cloned.1.call-update) | async-done | bytes 2097168 | tf_op jit(solution)/shard_map/all_gather | solution.py:201
  301.5 2.3 gather_fusion
  308.2 65.6 %all-gather.25.cloned.1.call-done = f32[64,128,128]{2,1,0:T(8,128)} async-done(((f32[2,128,128]{2,1,0:T(8,128)}), f32[64,128,128]{2,1,0:T(8,128)}) %all-gather.25.cloned.1.call-update) | async-done | bytes 4194320 | tf_op jit(solution)/shard_map/all_gather | solution.py:20
  373.9 5.6 copy.184
  379.5 4.6 rev.7
  384.1 62.6 %all-gather.23.cloned.1.call-done = f32[64,128,128]{2,1,0:T(8,128)} async-done(((f32[2,128,128]{2,1,0:T(8,128)}), f32[64,128,128]{2,1,0:T(8,128)}) %all-gather.23.cloned.1.call-update) | async-done | bytes 4194320 | tf_op jit(solution)/shard_map/all_gather | solution.py:20
  446.7 5.6 copy.180
  452.3 4.7 rev.6
  456.9 40.1 %while.175 = (s32[]{:T(128)}, f32[2,128,128]{1,2,0:T(8,128)S(1)}, s32[]{:T(128)}, f32[32,2,128,128]{2,3,1,0:T(8,128)}, f32[32,2,128,128]{2,3,1,0:T(8,128)}, /*index=5*/s32[]{:T(128)}, s32[]{:T(128)}) while((s32[]{:T(128)}, f32[2,128,128]{1,2,0:T(8,128)S(1)}, s32[]{:T(128)}, f32[32,2,128,128]{2,3,1,0:T(8,128)}, ...), condition=%wide.region_15.18_spmd.clone, body=%wide.region_14.17_spmd.clone.sunk | while | flops 50462724 | bytes 920159 | solution.py:32
  497.2 21.8 %all-gather.29.cloned.1.call-done = f32[64,128,128]{2,1,0:T(8,128)} async-done(((f32[2,128,128]{2,1,0:T(8,128)}), f32[64,128,128]{2,1,0:T(8,128)}) %all-gather.29.cloned.1.call-update) | async-done | bytes 4194320 | tf_op jit(solution)/shard_map/all_gather | solution.py:20
  519.0 72.6 %all-gather.27.cloned.1.call-done = f32[64,128,128]{2,1,0:T(8,128)} async-done(((f32[2,128,128]{2,1,0:T(8,128)}), f32[64,128,128]{2,1,0:T(8,128)}) %all-gather.27.cloned.1.call-update) | async-done | bytes 4194320 | tf_op jit(solution)/shard_map/all_gather | solution.py:20
  591.6 73.7 %while.176 = (s32[]{:T(128)}, f32[2,128,128]{1,2,0:T(8,128)S(1)}, s32[]{:T(128)}, f32[32,2,128,128]{3,2,1,0:T(8,128)}, f32[32,2,128,128]{3,2,1,0:T(8,128)}, /*index=5*/s32[]{:T(128)}, s32[]{:T(128)}) while((s32[]{:T(128)}, f32[2,128,128]{1,2,0:T(8,128)S(1)}, s32[]{:T(128)}, f32[32,2,128,128]{3,2,1,0:T(8,128)}, ...), condition=%wide.region_17.20_spmd.clone, body=%wide.region_16.19_spmd.clone.sunk | while | flops 50462724 | bytes 1443939 | solution.py:32
  606.9 1.3 fusion.512
  611.7 1.3 fusion.512
  635.5 1.3 fusion.512
  640.2 1.3 fusion.512
  642.6 1.3 fusion.512
  664.0 1.3 fusion.512
  666.0 28.2 %while.172 = (s32[]{:T(128)}, f32[2,128,128]{2,1,0:T(8,128)S(1)}, f32[2,2,64,64]{3,2,1,0:T(8,128)S(1)}, f32[2,2,64,64]{3,2,1,0:T(8,128)S(1)}, f32[2,2,64,64]{3,2...) while((s32[]{:T(128)}, f32[2,128,128]{2,1,0:T(8,128)S(1)}, ...), condition=%wide.region_20.23_spmd.clone.clone, body=%wide.region_18.22_spmd.clone.clone.sunk | while | flops 113643840 | bytes 2896269 | solution.py:92
  667.4 9.8 %custom-call.44 = f32[2,1,64,64]{2,3,1,0:T(8,128)S(1)} custom-call(f32[2,1,64,64]{3,2,1,0:T(8,128)S(1)} %add_bitcast_fusion.6), custom_call_target="InvertDiagBlocksLowerTriangular" | custom-call | tf_op jit(solution)/shard_map/jvp()/while/body/eval_jaxpr/triangular_solve/custom-call.1 | solution.py:54
  681.4 9.8 %custom-call.44 = f32[2,1,64,64]{2,3,1,0:T(8,128)S(1)} custom-call(f32[2,1,64,64]{3,2,1,0:T(8,128)S(1)} %add_bitcast_fusion.6), custom_call_target="InvertDiagBlocksLowerTriangular" | custom-call | tf_op jit(solution)/shard_map/jvp()/while/body/eval_jaxpr/triangular_solve/custom-call.1 | solution.py:54
  694.3 54.4 %while.173 = (s32[]{:T(128)}, f32[2,128,128]{2,1,0:T(8,128)S(1)}, f32[2,2,64,128]{3,2,1,0:T(8,128)S(1)}, f32[2,2,64,128]{3,2,1,0:T(8,128)S(1)}, f32[2,2,64,128]{...) while((s32[]{:T(128)}, f32[2,128,128]{2,1,0:T(8,128)S(1)}, ...), condition=%wide.region_32.35_spmd.clone.clone, body=%wide.region_21.34_spmd.clone.clone.sunk | while | flops 258757312 | bytes 5322969 | solution.py:92
  695.7 9.8 %custom-call.46 = f32[2,1,64,64]{2,3,1,0:T(8,128)S(1)} custom-call(f32[2,1,64,64]{3,2,1,0:T(8,128)S(1)} %add_bitcast_fusion.7), custom_call_target="InvertDiagBlocksLowerTriangular" | custom-call | tf_op jit(solution)/shard_map/transpose(jvp())/while/body/eval_jaxpr/triangular_solve | solution.py:54
  706.0 9.8 %custom-call.45 = f32[2,1,64,64]{2,3,1,0:T(8,128)S(1)} custom-call(f32[2,1,64,64]{3,2,1,0:T(8,128)S(1)} %fusion.479), custom_call_target="InvertDiagBlocksLowerTriangular" | custom-call | tf_op jit(solution)/shard_map/transpose(jvp())/while/body/eval_jaxpr/triangular_solve/custom-call.0 | solution.py:54
  722.9 9.8 %custom-call.46 = f32[2,1,64,64]{2,3,1,0:T(8,128)S(1)} custom-call(f32[2,1,64,64]{3,2,1,0:T(8,128)S(1)} %add_bitcast_fusion.7), custom_call_target="InvertDiagBlocksLowerTriangular" | custom-call | tf_op jit(solution)/shard_map/transpose(jvp())/while/body/eval_jaxpr/triangular_solve | solution.py:54
  733.2 9.8 %custom-call.45 = f32[2,1,64,64]{2,3,1,0:T(8,128)S(1)} custom-call(f32[2,1,64,64]{3,2,1,0:T(8,128)S(1)} %fusion.479), custom_call_target="InvertDiagBlocksLowerTriangular" | custom-call | tf_op jit(solution)/shard_map/transpose(jvp())/while/body/eval_jaxpr/triangular_solve/custom-call.0 | solution.py:54
  749.7 1.3 fusion.302
  751.1 1.3 fusion.299
  754.7 1.3 add_add_fusion
  756.0 1.4 add_add_fusion.1
  757.4 1.7 copy.420
  759.1 1.7 copy.421
  (584 shorter events, 171.7 us)
Async XLA Ops:
  7.2 95.0 %all-gather.15.cloned.1.call-start = ((), (), s32[]{:S(2)}) async-start(), calls=%async_computation | async-start | bytes 2162688 | tf_op jit(solution)/shard_map/all_gather | solution.py:228
  7.9 151.0 %all-gather.17.cloned.1.call-start = ((), (), s32[]{:S(2)}) async-start(), calls=%async_computation.1 | async-start | bytes 2162688 | tf_op jit(solution)/shard_map/all_gather | solution.py:231
  8.7 223.0 %all-gather.21.cloned.1.call-start = ((), (), s32[]{:S(2)}) async-start(), calls=%async_computation.3 | async-start | bytes 2162688 | tf_op jit(solution)/shard_map/all_gather | solution.py:202
  10.4 291.1 %all-gather.19.cloned.1.call-start = ((), (), s32[]{:S(2)}) async-start(), calls=%async_computation.2 | async-start | bytes 2162688 | tf_op jit(solution)/shard_map/all_gather | solution.py:201
  12.2 361.7 %all-gather.25.cloned.1.call-start = ((), (), s32[]{:S(2)}) async-start(), calls=%async_computation.5 | async-start | bytes 4325376 | tf_op jit(solution)/shard_map/all_gather | solution.py:20
  13.2 1.4 copy-start.28
  13.8 3.2 copy-start.23
  15.5 0.6 copy-start.27
  16.1 1.5 copy-start.24
  17.6 0.8 copy-start.25
  20.4 24.5 %copy-start.19 = (bf16[128,256]{1,0:T(8,128)(2,1)S(1)}, bf16[128,256]{1,0:T(8,128)(2,1)}, u32[]{:S(2)}) copy-start(bf16[128,256]{1,0:T(8,128)(2,1)} %param.47) | copy-start | bytes 196612
  44.8 0.7 copy-start.2
  69.0 0.6 copy-start.1
  69.7 377.0 %all-gather.23.cloned.1.call-start = ((), (), s32[]{:S(2)}) async-start(), calls=%async_computation.4 | async-start | bytes 4325376 | tf_op jit(solution)/shard_map/all_gather | solution.py:20
  69.8 26.5 %copy-start.5 = (bf16[128,1,256]{0,2,1:T(8,128)(2,1)S(1)}, bf16[128,1,256]{0,2,1:T(8,128)(2,1)}, u32[]{:S(2)}) copy-start(bf16[128,1,256]{0,2,1:T(8,128)(2,1)} %constant_dynamic-slice_fusion.18) | copy-start | bytes 196612
  69.8 26.6 %copy-start.21 = (s32[1,64,4]{1,2,0:T(4,128)S(1)}, s32[1,64,4]{1,2,0:T(4,128)}, u32[]{:S(2)}) copy-start(s32[1,64,4]{1,2,0:T(4,128)} %param.39) | copy-start | bytes 3076
  69.8 27.8 %copy-start.31 = (f32[1,4096]{1,0:T(1,128)S(1)}, f32[1,4096]{1,0:T(1,128)}, u32[]{:S(2)}) copy-start(f32[1,4096]{1,0:T(1,128)} %param.37) | copy-start | bytes 49156
  69.8 27.9 %copy-start.20 = (f32[1,4096]{1,0:T(1,128)S(1)}, f32[1,4096]{1,0:T(1,128)}, u32[]{:S(2)}) copy-start(f32[1,4096]{1,0:T(1,128)} %param.38) | copy-start | bytes 49156
  69.8 31.3 %copy-start.6 = (bf16[128,1,256]{2,0,1:T(8,128)(2,1)S(1)}, bf16[128,1,256]{2,0,1:T(8,128)(2,1)}, u32[]{:S(2)}) copy-start(bf16[128,1,256]{2,0,1:T(8,128)(2,1)} %copy.214) | copy-start | bytes 196612
  69.9 31.3 %copy-start.15 = (bf16[128,256]{1,0:T(8,128)(2,1)S(1)}, bf16[128,256]{1,0:T(8,128)(2,1)}, u32[]{:S(2)}) copy-start(bf16[128,256]{1,0:T(8,128)(2,1)} %param.33) | copy-start | bytes 196612
  69.9 31.5 %copy-start.8 = (bf16[128,256]{1,0:T(8,128)(2,1)S(1)}, bf16[128,256]{1,0:T(8,128)(2,1)}, u32[]{:S(2)}) copy-start(bf16[128,256]{1,0:T(8,128)(2,1)} %param.36) | copy-start | bytes 196612
  93.6 1.6 copy-start
  93.6 2.3 copy-start.12
  93.6 2.3 copy-start.17
  94.4 424.6 %all-gather.29.cloned.1.call-start = ((), (), s32[]{:S(2)}) async-start(), calls=%async_computation.7 | async-start | bytes 4325376 | tf_op jit(solution)/shard_map/all_gather | solution.py:20
  95.2 496.5 %all-gather.27.cloned.1.call-start = ((), (), s32[]{:S(2)}) async-start(), calls=%async_computation.6 | async-start | bytes 4325376 | tf_op jit(solution)/shard_map/all_gather | solution.py:20
  95.9 661.5 %all-reduce.5.cloned.1.call-start = ((), (), s32[]{:S(2)}) async-start(), calls=%async_computation.8 | async-start | bytes 1048576 | tf_op jit(solution)/shard_map/psum | solution.py:254
  97.7 4.4 copy-start.26
  97.8 4.3 copy-start.22
  158.9 2.6 copy-start.4
  161.5 1.6 copy-start.3
  165.2 139.7 %copy-start.9 = (bf16[128,256]{1,0:T(8,128)(2,1)S(1)}, bf16[128,256]{1,0:T(8,128)(2,1)}, u32[]{:S(2)}) copy-start(bf16[128,256]{1,0:T(8,128)(2,1)} %param.36) | copy-start | bytes 196612
  236.3 70.2 %copy-start.16 = (f32[2,64,64]{1,2,0:T(8,128)S(1)}, f32[2,64,64]{1,2,0:T(8,128)}, u32[]{:S(2)}) copy-start(f32[2,64,64]{1,2,0:T(8,128)} %fusion.283) | copy-start | bytes 98308
  236.3 71.1 %copy-start.7 = (f32[16,8,2,256]{3,1,2,0:T(8,128)S(1)}, f32[16,8,2,256]{3,1,2,0:T(8,128)}, u32[]{:S(2)}) copy-start(f32[16,8,2,256]{3,1,2,0:T(8,128)} %copy.217) | copy-start | bytes 786436
  236.3 71.1 %copy-start.30 = (pred[512]{0:T(512)(128)(4,1)S(1)}, pred[512]{0:T(512)(128)(4,1)}, u32[]{:S(2)}) copy-start(pred[512]{0:T(512)(128)(4,1)} %broadcast_in_dim.479) | copy-start | bytes 1540
  665.3 0.7 copy-start.13
  665.3 0.7 copy-start.18
  666.0 28.2 %copy-start.14 = (pred[64,64]{1,0:T(8,128)(4,1)S(1)}, pred[64,64]{1,0:T(8,128)(4,1)}, u32[]{:S(2)}) copy-start(pred[64,64]{1,0:T(8,128)(4,1)} %iota_compare_fusion.16) | copy-start | bytes 12292
  694.2 54.5 %copy-start.10 = (bf16[128,128]{1,0:T(8,128)(2,1)S(1)}, bf16[128,128]{1,0:T(8,128)(2,1)}, u32[]{:S(2)}) copy-start(bf16[128,128]{1,0:T(8,128)(2,1)} %param.41) | copy-start | bytes 98308
  694.3 55.3 %copy-start.29 = (f32[128]{0:T(128)S(1)}, f32[128]{0:T(128)}, u32[]{:S(2)}) copy-start(f32[128]{0:T(128)} %copy-done.28) | copy-start | bytes 1540
  694.3 58.2 %copy-start.11 = (bf16[128,128]{1,0:T(8,128)(2,1)S(1)}, bf16[128,128]{1,0:T(8,128)(2,1)}, u32[]{:S(2)}) copy-start(bf16[128,128]{1,0:T(8,128)(2,1)} %param.40) | copy-start | bytes 98308
  694.3 22.1 %copy-start.32 = (f32[2,2,1,1]{1,3,2,0:T(1,128)}, f32[2,2,1,1]{1,3,2,0:T(1,128)S(1)}, u32[]{:S(2)}) copy-start(f32[2,2,1,1]{1,3,2,0:T(1,128)S(1)} %get-tuple-element.4409) | copy-start | bytes 52 | tf_op jit(solution)/shard_map/transpose(jvp())/while
  717.5 4.0 copy-start.33
  721.5 22.1 %copy-start.32 = (f32[2,2,1,1]{1,3,2,0:T(1,128)}, f32[2,2,1,1]{1,3,2,0:T(1,128)S(1)}, u32[]{:S(2)}) copy-start(f32[2,2,1,1]{1,3,2,0:T(1,128)S(1)} %get-tuple-element.4409) | copy-start | bytes 52 | tf_op jit(solution)/shard_map/transpose(jvp())/while
  744.7 4.0 copy-start.33
Sparse Core Ops, SparseCore 0:
  10.1 79.2 all-gather.14
  91.5 67.3 all-gather.16
  161.5 70.0 all-gather.20
  234.2 67.3 all-gather.18
  303.5 70.3 all-gather.24
  376.4 70.1 all-gather.22
  448.8 70.1 all-gather.28
  521.1 70.4 all-gather.26
  595.5 111.3 all-reduce.4
where the time goes:
time: 770 us; the launch traced here: 767 us
  waiting for transfers between devices  411 us (53%)
  other arithmetic  142 us (18%)
  matrix products  114 us (15%)
  local copies, waits for them, and re-layouts  80.6 us (10%)
  between operations  14.9 us (2%)
    all_gather x4, waiting for transfers between devices, prefix(): pieces = jax.tree.map(lambda part: lax.all_gather(part, axis), value)  223 us
    another operation x44, other arithmetic, span_update(): lax.linalg.triangular_solve(system, target, left_side=True, lower=True, u...  119 us
    dot_general x62, matrix products, compose_maps(): jnp.einsum('hij,hjk->hik', earlier[1], later[0], precision=HIGHEST)  79.1 us
    all_gather x1, waiting for transfers between devices, on_device(): lax.all_gather(own_values, 'ctx', axis=0, tiled=True)  66.4 us
    all_gather x1, waiting for transfers between devices, on_device(): lax.all_gather(own_keys, 'ctx', axis=0, tiled=True)  65.2 us
    all_gather x1, waiting for transfers between devices, on_device(): lax.all_gather(attn_cot, 'ctx', axis=0, tiled=True)  53.9 us
    dynamic_slice x62, local copies, waits for them, and re-layouts, turn(): longer = join(so_far, jax.tree.map(lambda part: part[position], pieces))  31.4 us
  transfers between devices with their start and end apart: 9, of which 7 were waited for; matrix products, arithmetic and copies ran while one was open for 43% of the time, Pallas kernels for 0%

commit v1 on v0

--- a/solution.py
+++ b/solution.py
@@ -15,21 +15,32 @@
 HIGHEST = lax.Precision.HIGHEST
 
 
-def prefix(value, axis, join, neutral, backward):
+def shifted(value, axis, step, backward):
+    count = lax.axis_size(axis)
+    if backward:
+        pairs = [(i + step, i) for i in range(count - step)]
+    else:
+        pairs = [(i, i + step) for i in range(count - step)]
+    return jax.tree.map(lambda part: lax.ppermute(part, axis, pairs), value)
+
+
+def exclusive_scans(forward, backward, axis, join):
     count, mine = (lax.axis_size(axis), lax.axis_index(axis))
-    pieces = jax.tree.map(lambda part: lax.all_gather(part, axis), value)
-    if backward:
-        pieces = jax.tree.map(lambda part: part[::-1], pieces)
-        mine = count - 1 - mine
-    so_far = jax.tree.map(
-        lambda part, zero: jnp.full_like(part, 0) + jnp.asarray(zero, part.dtype), value, neutral
-    )
-
-    def turn(position, so_far):
-        longer = join(so_far, jax.tree.map(lambda part: part[position], pieces))
-        return jax.tree.map(lambda new, old: jnp.where(position < mine, new, old), longer, so_far)
-
-    return lax.fori_loop(0, count - 1, turn, so_far)
+    step = 1
+    while step < count:
+        last = 2 * step >= count
+        if last:
+            got_f = (None, shifted(forward[1], axis, step, False))
+            got_b = (None, shifted(backward[1], axis, step, True))
+        else:
+            got_f = shifted(forward, axis, step, False)
+            got_b = shifted(backward, axis, step, True)
+        new_f = join(got_f, forward, last)
+        new_b = join(got_b, backward, last)
+        forward = jax.tree.map(lambda n, o: jnp.where(mine >= step, n, o), new_f, forward)
+        backward = jax.tree.map(lambda n, o: jnp.where(mine + step < count, n, o), new_b, backward)
+        step *= 2
+    return (shifted(forward[1], axis, 1, False), shifted(backward[1], axis, 1, True))
 
 
 def unit_rows(matrix):
@@ -154,10 +165,12 @@
     return (own_part + list_part) * score_scale
 
 
-def compose_maps(earlier, later):
+def compose_maps(earlier, later, last=False):
+    shifted_part = jnp.einsum("hij,hjk->hik", earlier[1], later[0], precision=HIGHEST) + later[1]
+    if last:
+        return (later[0], shifted_part)
     product = jnp.einsum("hij,hjk->hik", earlier[0], later[0], precision=HIGHEST)
-    shifted = jnp.einsum("hij,hjk->hik", earlier[1], later[0], precision=HIGHEST) + later[1]
-    return (product, shifted)
+    return (product, shifted_part)
 
 
 def on_device(
@@ -197,10 +210,10 @@
     member_rows = jnp.repeat(jnp.repeat(member, BLK, axis=1), BLK, axis=2)
     key_pos = row_base + jnp.arange(tok_rows, dtype=jnp.int32)
     key_block = key_pos // BLK
-    keys_whole, values_whole = (
-        lax.all_gather(own_keys, "ctx", axis=0, tiled=True),
-        lax.all_gather(own_values, "ctx", axis=0, tiled=True),
-    )
+    packed = jnp.concatenate([own_keys, own_values, attn_q, attn_cot], axis=1)
+    gathered = lax.all_gather(packed, "ctx", axis=0, tiled=True)
+    keys_whole = gathered[:, :HD]
+    values_whole = gathered[:, HD : 2 * HD]
     lists_own = lax.dynamic_slice_in_dim(block_lists, first_block, blocks_here, 1)
     lse_own = lax.dynamic_slice_in_dim(attn_lse, row_base, tok_rows, 1).reshape(
         local_heads, blocks_here, BLK
@@ -225,10 +238,10 @@
         key_block_ids,
     )
     grad_q = grad_blocks.transpose(1, 2, 0, 3).reshape(tok_rows, local_heads * HD)
-    query_rows = lax.all_gather(attn_q, "ctx", axis=0, tiled=True)
-    n_rows = query_rows.shape[0]
-    queries = query_rows.reshape(n_rows, local_heads, HD)
-    cotangent = lax.all_gather(attn_cot, "ctx", axis=0, tiled=True).reshape(n_rows, local_heads, HD)
+    width = local_heads * HD
+    n_rows = gathered.shape[0]
+    queries = gathered[:, 2 * HD : 2 * HD + width].reshape(n_rows, local_heads, HD)
+    cotangent = gathered[:, 2 * HD + width :].reshape(n_rows, local_heads, HD)
     row_pos = jnp.arange(n_rows, dtype=jnp.int32)
     row_block = row_pos // BLK
     own_pair = (row_block[:, None] == key_block[None, :]) & (row_pos[:, None] >= key_pos[None, :])
@@ -278,13 +291,12 @@
     written_end = outputs_zero[1]
     cot_full = gdn_cot.astype(jnp.float32)
     local_grad = pull_zero((cot_full, zero_memory))[1]
-    memory_in = prefix(
-        (transition, written_end), "ctx", compose_maps, (unit_memory, zero_memory), False
-    )[1]
-    flipped = jnp.swapaxes(transition, 1, 2)
-    memory_grad = prefix(
-        (flipped, local_grad), "ctx", compose_maps, (unit_memory, zero_memory), True
-    )[1]
+    memory_in, memory_grad = exclusive_scans(
+        (transition, written_end),
+        (jnp.swapaxes(transition, 1, 2), local_grad),
+        "ctx",
+        compose_maps,
+    )
     unused_out, pull_final = jax.vjp(local_run, raw_inputs, memory_in)
     grads = pull_final((cot_full, memory_grad))[0]
     return (grad_q, attn_dk, attn_dv, grads[0], grads[1], grads[2], grads[3], grads[4])

time: 770 us -> 471 us (0.61)
  waiting for transfers between devices: 411 us -> 128 us
  starting transfers between devices: 0.54 us -> 87 us
  matrix products: 114 us -> 42.7 us
  local copies, waits for them, and re-layouts: 80.6 us -> 47.7 us
    all_gather x8 -> x1, waiting for transfers between devices: 408 us -> 0.02 us  [on_device(): gathered = lax.all_gather(packed, 'ctx', axis=0, tiled=True)]
    psum x1, waiting for transfers between devices: 0.01 us -> 122 us  [on_device(): attn_dk, attn_dv = lax.psum((key_slots, value_slots), 'head')]
    ppermute x0 -> x20, starting transfers between devices: none -> 86.9 us  [shifted(): return jax.tree.map(lambda part: lax.ppermute(part, axis, pairs), value)]
    dot_general x62 -> x10, matrix products: 79.1 us -> 3.47 us  [compose_maps(): jnp.einsum('hij,hjk->hik', earlier[1], later[0], precision=HIGHEST)]
    dynamic_slice x64 -> x0, local copies, waits for them, and re-layouts: 31.6 us -> none  [the longest x62 31.4 us: turn(): longer = join(so_far, jax.tree.map(lambda part: part[position], pieces))]
    all_gather x3 -> x0, local copies, waits for them, and re-layouts: 14.5 us -> none  [the longest x2 11.2 us: prefix(): pieces = jax.tree.map(lambda part: lax.all_gather(part, axis), value)]
    rev x2 -> x0, local copies, waits for them, and re-layouts: 9.27 us -> none  [prefix(): pieces = jax.tree.map(lambda part: part[::-1], pieces)]
  transfers between devices with their start and end apart: 9 -> 22, of which waited for: 7 -> 3; matrix products, arithmetic and copies ran while one was open for 43% -> 46% of each run, Pallas kernels for 0% -> 0%
where the time goes in v1:
time: 471 us; the launch traced here: 468 us
  other arithmetic  146 us (31%)
  waiting for transfers between devices  128 us (27%)
  starting transfers between devices  87 us (18%)
  local copies, waits for them, and re-layouts  47.7 us (10%)
  matrix products  42.7 us (9%)
  between operations  15.4 us (3%)
    psum x1, waiting for transfers between devices, on_device(): attn_dk, attn_dv = lax.psum((key_slots, value_slots), 'head')  122 us
    another operation x44, other arithmetic, span_update(): lax.linalg.triangular_solve(system, target, left_side=True, lower=True, u...  119 us
    ppermute x20, starting transfers between devices, shifted(): return jax.tree.map(lambda part: lax.ppermute(part, axis, pairs), value)  86.9 us
  transfers between devices with their start and end apart: 22, of which 3 were waited for; matrix products, arithmetic and copies ran while one was open for 46% of the time, Pallas kernels for 0%

profile of v1, /device:TPU:1, one launch (start us, length us, event | category | flops | bytes accessed | tf_op | source)
XLA Modules:
  0.0 468.4 jit_solution(16589709241327713699)
XLA Ops:
  9.5 1.6 pad_maximum_fusion
  14.5 25.8 %while.147 = (s32[]{:T(128)}, f32[2,128,128]{2,1,0:T(8,128)S(1)}, f32[2,2,64,1]{2,1,3,0:T(2,128)S(1)}, f32[2,2,64,1]{2,1,3,0:T(2,128)S(1)}, f32[2,2,64,64]{3,2,1...) while((s32[]{:T(128)}, f32[2,128,128]{2,1,0:T(8,128)S(1)}, ...), condition=%wide.region_8.10_spmd.clone.clone, body=%wide.region_6.9_spmd.clone.clone.sunk | while | flops 88404160 | bytes 1474303 | solution.py:103
  16.5 9.8 %custom-call.46 = f32[2,1,64,64]{2,3,1,0:T(8,128)S(1)} custom-call(f32[2,1,64,64]{3,2,1,0:T(8,128)S(1)} %add_bitcast_fusion.8), custom_call_target="InvertDiagBlocksLowerTriangular" | custom-call | tf_op jit(solution)/shard_map/jvp()/while/body/eval_jaxpr/triangular_solve/custom-call.1 | solution.py:65
  29.4 9.8 %custom-call.46 = f32[2,1,64,64]{2,3,1,0:T(8,128)S(1)} custom-call(f32[2,1,64,64]{3,2,1,0:T(8,128)S(1)} %add_bitcast_fusion.8), custom_call_target="InvertDiagBlocksLowerTriangular" | custom-call | tf_op jit(solution)/shard_map/jvp()/while/body/eval_jaxpr/triangular_solve/custom-call.1 | solution.py:65
  40.4 23.6 %while.146 = (s32[]{:T(128)}, f32[2,128,128]{2,1,0:T(8,128)S(1)}, f32[2,2,1,1]{1,3,2,0:T(1,128)S(1)}, f32[2,2,64,1]{2,1,3,0:T(2,128)S(1)}, f32[2,2,64,128]{3,2,1...) while((s32[]{:T(128)}, f32[2,128,128]{2,1,0:T(8,128)S(1)}, ...), condition=%wide.region_10.13_spmd.clone, body=%wide.region_9.12_spmd.clone.sunk | while | flops 100954176 | bytes 1590979 | solution.py:103
  41.8 9.8 %custom-call.45 = f32[2,1,64,64]{2,3,1,0:T(8,128)S(1)} custom-call(f32[2,1,64,64]{3,2,1,0:T(8,128)S(1)} %fusion.532), custom_call_target="InvertDiagBlocksLowerTriangular" | custom-call | tf_op jit(solution)/shard_map/transpose(jvp())/while/body/eval_jaxpr/triangular_solve/custom-call.0 | solution.py:65
  53.6 9.8 %custom-call.45 = f32[2,1,64,64]{2,3,1,0:T(8,128)S(1)} custom-call(f32[2,1,64,64]{3,2,1,0:T(8,128)S(1)} %fusion.532), custom_call_target="InvertDiagBlocksLowerTriangular" | custom-call | tf_op jit(solution)/shard_map/transpose(jvp())/while/body/eval_jaxpr/triangular_solve/custom-call.0 | solution.py:65
  64.0 8.7 %collective-permute-start = (f32[2,128,128]{2,1,0:T(8,128)S(1)}, f32[2,128,128]{2,1,0:T(8,128)S(1)}, u32[]{:S(2)}, u32[]{:S(2)}) collective-permute-start(f32[2,128,128]{2,1,0:T(8,128)S(1)} %get-tuple-element.1862), channel_id=1, source_target_pairs={{16,0},{32,16},{48,32},{64,48},{80,64},{96,80},{112,96},{128,112},... | collective-permute-start | bytes 393224 | tf_op jit(solution)/shard_map/ppermute | solution.py:24
  72.9 25.1 %while.143 = (s32[]{:T(128)}, f32[2,128,128]{2,1,0:T(8,128)S(1)}, f32[2,2,64]{2,1,0:T(2,128)}, f32[2,2,64]{2,1,0:T(2,128)S(1)}, f32[2,2,64,128]{3,2,1,0:T(8,128)S(1)}, /*index=5*/s32[]{:T(128)}, f32[]{:T(128)}) while((s32[]{:T(128)}, f32[2,128,128]{2,1,0:T(8,128)S(1)}, f32[2,2,64]{2,1,0:T(2,128)}, f32[2,2,64]{2,1,0:T(2,128)S(1)}, ...), condition=%wide.region_13.16_spmd, body=%wide.region_11.15_spmd.sunk | while | flops 75726912 | bytes 1051793 | solution.py:103
  74.8 9.8 %custom-call.41 = f32[2,1,64,64]{2,3,1,0:T(8,128)S(1)} custom-call(f32[2,1,64,64]{3,2,1,0:T(8,128)S(1)} %fusion.467), custom_call_target="InvertDiagBlocksLowerTriangular" | custom-call | tf_op jit(solution)/shard_map/while/body/eval_jaxpr/triangular_solve/custom-call.1 | solution.py:65
  87.3 9.9 %custom-call.41 = f32[2,1,64,64]{2,3,1,0:T(8,128)S(1)} custom-call(f32[2,1,64,64]{3,2,1,0:T(8,128)S(1)} %fusion.467), custom_call_target="InvertDiagBlocksLowerTriangular" | custom-call | tf_op jit(solution)/shard_map/while/body/eval_jaxpr/triangular_solve/custom-call.1 | solution.py:65
  97.9 1.9 collective-permute-start.12
  100.0 2.4 collective-permute-start.2
  102.4 3.2 collective-permute-start.10
  114.3 1.3 collective-permute-start.4
  115.9 4.6 collective-permute-start.11
  120.8 3.4 collective-permute-start.14
  124.4 1.3 collective-permute-start.3
  126.0 1.3 collective-permute-start.6
  127.6 6.1 %collective-permute-start.13 = (f32[2,128,128]{2,1,0:T(8,128)S(1)}, f32[2,128,128]{2,1,0:T(8,128)S(1)}, u32[]{:S(2)}, u32[]{:S(2)}) collective-permute-start(f32[2,128,128]{2,1,0:T(8,128)S(1)} %fusion.272), channel_id=1, source_target_pairs={{0,64},{16,80},{32,96},{48,112},{64,128},{80,144},{96,160},{112,17... | collective-permute-start | bytes 393224 | tf_op jit(solution)/shard_map/ppermute | solution.py:24
  134.1 5.5 %collective-permute-start.16 = (f32[2,128,128]{2,1,0:T(8,128)S(1)}, f32[2,128,128]{2,1,0:T(8,128)S(1)}, u32[]{:S(2)}, u32[]{:S(2)}) collective-permute-start(f32[2,128,128]{2,1,0:T(8,128)S(1)} %convolution_select_fusion.2), channel_id=1, source_target_pairs={{0,64},{16,80},{32,96},{48,112},{64,128},{80,144},{96,160},{112,17... | collective-permute-start | bytes 393224 | tf_op jit(solution)/shard_map/ppermute | solution.py:24
  139.8 1.3 collective-permute-start.5
  143.0 10.1 %collective-permute-start.15 = (f32[2,128,128]{2,1,0:T(8,128)S(1)}, f32[2,128,128]{2,1,0:T(8,128)S(1)}, u32[]{:S(2)}, u32[]{:S(2)}) collective-permute-start(f32[2,128,128]{2,1,0:T(8,128)S(1)} %fusion.271), channel_id=1, source_target_pairs={{0,128},{16,144},{32,160},{48,176},{64,192},{80,208},{96,224},{112... | collective-permute-start | bytes 393224 | tf_op jit(solution)/shard_map/ppermute | solution.py:24
  153.4 7.3 %collective-permute-start.18 = (f32[2,128,128]{2,1,0:T(8,128)S(1)}, f32[2,128,128]{2,1,0:T(8,128)S(1)}, u32[]{:S(2)}, u32[]{:S(2)}) collective-permute-start(f32[2,128,128]{2,1,0:T(8,128)S(1)} %convolution_select_fusion.1), channel_id=1, source_target_pairs={{0,128},{16,144},{32,160},{48,176},{64,192},{80,208},{96,224},{112... | collective-permute-start | bytes 393224 | tf_op jit(solution)/shard_map/ppermute | solution.py:24
  160.9 1.3 collective-permute-start.7
  162.5 18.8 %collective-permute-start.17 = (f32[2,128,128]{2,1,0:T(8,128)S(1)}, f32[2,128,128]{2,1,0:T(8,128)S(1)}, u32[]{:S(2)}, u32[]{:S(2)}) collective-permute-start(f32[2,128,128]{2,1,0:T(8,128)S(1)} %fusion.270), channel_id=1, source_target_pairs={{0,256},{16,272},{32,288},{48,304},{64,320},{80,336},{96,352},{112... | collective-permute-start | bytes 393224 | tf_op jit(solution)/shard_map/ppermute | solution.py:24
  183.3 1.9 collective-permute-start.19
  185.2 4.7 %collective-permute-done.7 = f32[2,128,128]{2,1,0:T(8,128)S(1)} collective-permute-done((f32[2,128,128]{2,1,0:T(8,128)S(1)}, f32[2,128,128]{2,1,0:T(8,128)S(1)}, u32[]{:S(2)}, u32[]{:S(2)}) %collective-permute-start.7) | collective-permute-done | bytes 131104 | tf_op jit(solution)/shard_map/ppermute | solution.py:24
  190.9 4.0 collective-permute-start.9
  198.6 37.7 %while.144 = (s32[]{:T(128)}, f32[2,128,128]{2,1,0:T(8,128)S(1)}, f32[2,2,64,64]{3,2,1,0:T(8,128)S(1)}, f32[2,2,64,64]{3,2,1,0:T(8,128)S(1)}, f32[2,2,64,64]{3,2...) while((s32[]{:T(128)}, f32[2,128,128]{2,1,0:T(8,128)S(1)}, ...), condition=%wide.region_16.19_spmd.clone.clone, body=%wide.region_14.18_spmd.clone.clone.sunk | while | flops 113643840 | bytes 2893229 | solution.py:103
  202.1 9.8 %custom-call.42 = f32[2,1,64,64]{2,3,1,0:T(8,128)S(1)} custom-call(f32[2,1,64,64]{3,2,1,0:T(8,128)S(1)} %add_bitcast_fusion.6), custom_call_target="InvertDiagBlocksLowerTriangular" | custom-call | tf_op jit(solution)/shard_map/jvp()/while/body/eval_jaxpr/triangular_solve/custom-call.1 | solution.py:65
  220.9 9.8 %custom-call.42 = f32[2,1,64,64]{2,3,1,0:T(8,128)S(1)} custom-call(f32[2,1,64,64]{3,2,1,0:T(8,128)S(1)} %add_bitcast_fusion.6), custom_call_target="InvertDiagBlocksLowerTriangular" | custom-call | tf_op jit(solution)/shard_map/jvp()/while/body/eval_jaxpr/triangular_solve/custom-call.1 | solution.py:65
  238.8 66.9 %while.145 = (s32[]{:T(128)}, f32[2,128,128]{2,1,0:T(8,128)S(1)}, f32[2,2,64,128]{3,2,1,0:T(8,128)S(1)}, f32[2,2,64,128]{3,2,1,0:T(8,128)}, f32[2,2,64,128]{3,2,...) while((s32[]{:T(128)}, f32[2,128,128]{2,1,0:T(8,128)S(1)}, ...), condition=%wide.region_28.31_spmd.clone.clone, body=%wide.region_17.30_spmd.clone.clone.sunk | while | flops 258757312 | bytes 5292101 | solution.py:103
  243.8 9.8 %custom-call.43 = f32[2,1,64,64]{2,3,1,0:T(8,128)S(1)} custom-call(f32[2,1,64,64]{3,2,1,0:T(8,128)S(1)} %fusion.506), custom_call_target="InvertDiagBlocksLowerTriangular" | custom-call | tf_op jit(solution)/shard_map/transpose(jvp())/while/body/eval_jaxpr/triangular_solve/custom-call.0 | solution.py:65
  256.6 9.8 %custom-call.44 = f32[2,1,64,64]{2,3,1,0:T(8,128)S(1)} custom-call(f32[2,1,64,64]{3,2,1,0:T(8,128)S(1)} %add_bitcast_fusion.7), custom_call_target="InvertDiagBlocksLowerTriangular" | custom-call | tf_op jit(solution)/shard_map/transpose(jvp())/while/body/eval_jaxpr/triangular_solve | solution.py:65
  277.2 9.8 %custom-call.43 = f32[2,1,64,64]{2,3,1,0:T(8,128)S(1)} custom-call(f32[2,1,64,64]{3,2,1,0:T(8,128)S(1)} %fusion.506), custom_call_target="InvertDiagBlocksLowerTriangular" | custom-call | tf_op jit(solution)/shard_map/transpose(jvp())/while/body/eval_jaxpr/triangular_solve/custom-call.0 | solution.py:65
  290.0 9.8 %custom-call.44 = f32[2,1,64,64]{2,3,1,0:T(8,128)S(1)} custom-call(f32[2,1,64,64]{3,2,1,0:T(8,128)S(1)} %add_bitcast_fusion.7), custom_call_target="InvertDiagBlocksLowerTriangular" | custom-call | tf_op jit(solution)/shard_map/transpose(jvp())/while/body/eval_jaxpr/triangular_solve | solution.py:65
  312.7 1.3 fusion.300
  314.0 1.3 fusion.297
  315.4 1.4 add_add_fusion.1
  316.8 1.3 add_add_fusion
  318.1 3.9 fusion.306
  322.0 2.2 gather_fusion
  324.8 3.0 fusion.249
  327.8 2.9 fusion.254
  335.8 122.4 %all-reduce.5.cloned.1.call-done = (f32[128,512]{1,0:T(8,128)}, f32[128,512]{1,0:T(8,128)}) async-done(((f32[128,512]{1,0:T(8,128)}, f32[128,512]{1,0:T(8,128)}), (f32[128,512]{1,0:T(8,128)}, f32[128,512]{1,0:T(8,128)})) %all-reduce.5.cloned.1.call-update) | async-done | bytes 524304 | tf_op jit(solution)/shard_map/psum | solution.py:267
  458.2 1.7 copy.332
  459.9 1.7 copy.333
  (422 shorter events, 100.3 us)
Async XLA Ops:
  7.2 4.1 copy-start.20
  7.2 4.1 copy-start.17
  7.2 4.2 copy-start.31
  7.2 4.8 %copy-start.16 = (f32[2,128]{1,0:T(2,128)S(1)}, f32[2,128]{1,0:T(2,128)}, u32[]{:S(2)}) copy-start(f32[2,128]{1,0:T(2,128)} %param.39) | copy-start | bytes 3076
  7.2 4.9 %copy-start.3 = (bf16[128,128]{1,0:T(8,128)(2,1)S(1)}, bf16[128,128]{1,0:T(8,128)(2,1)}, u32[]{:S(2)}) copy-start(bf16[128,128]{1,0:T(8,128)(2,1)} %param.37) | copy-start | bytes 98308
  7.2 5.7 %copy-start.7 = (bf16[128,256]{1,0:T(8,128)(2,1)S(1)}, bf16[128,256]{1,0:T(8,128)(2,1)}, u32[]{:S(2)}) copy-start(bf16[128,256]{1,0:T(8,128)(2,1)} %param.38) | copy-start | bytes 196612
  7.2 5.8 %copy-start.2 = (bf16[128,128]{1,0:T(8,128)(2,1)S(1)}, bf16[128,128]{1,0:T(8,128)(2,1)}, u32[]{:S(2)}) copy-start(bf16[128,128]{1,0:T(8,128)(2,1)} %param.36) | copy-start | bytes 98308
  7.2 310.9 %all-gather.2.cloned.1.call-start = ((), (), s32[]{:S(2)}) async-start(), calls=%async_computation | async-start | bytes 8650752 | tf_op jit(solution)/shard_map/all_gather | solution.py:214
  11.2 447.0 %all-reduce.5.cloned.1.call-start = ((), (), s32[]{:S(2)}) async-start(), calls=%async_computation.1 | async-start | bytes 1048576 | tf_op jit(solution)/shard_map/psum | solution.py:267
  12.8 1.6 copy-start.18
  14.5 25.8 %copy-start.8 = (bf16[128,256]{1,0:T(8,128)(2,1)S(1)}, bf16[128,256]{1,0:T(8,128)(2,1)}, u32[]{:S(2)}) copy-start(bf16[128,256]{1,0:T(8,128)(2,1)} %param.43) | copy-start | bytes 196612
  64.0 48.1 %collective-permute-start = (f32[2,128,128]{2,1,0:T(8,128)S(1)}, f32[2,128,128]{2,1,0:T(8,128)S(1)}, u32[]{:S(2)}, u32[]{:S(2)}) collective-permute-start(f32[2,128,128]{2,1,0:T(8,128)S(1)} %get-tuple-element.1862), channel_id=1, source_target_pairs={{16,0},{32,16},{48,32},{64,48},{80,64},{96,80},{112,96},{128,112},... | collective-permute-start | bytes 393224 | tf_op jit(solution)/shard_map/ppermute | solution.py:24
  72.8 33.5 %copy-start.13 = (s32[1,64,4]{1,2,0:T(4,128)S(1)}, s32[1,64,4]{1,2,0:T(4,128)}, u32[]{:S(2)}) copy-start(s32[1,64,4]{1,2,0:T(4,128)} %param.35) | copy-start | bytes 3076
  72.8 35.6 %copy-start.4 = (bf16[128,256]{1,0:T(8,128)(2,1)S(1)}, bf16[128,256]{1,0:T(8,128)(2,1)}, u32[]{:S(2)}) copy-start(bf16[128,256]{1,0:T(8,128)(2,1)} %param.29) | copy-start | bytes 196612
  72.8 35.7 %copy-start.1 = (bf16[128,256]{1,0:T(8,128)(2,1)S(1)}, bf16[128,256]{1,0:T(8,128)(2,1)}, u32[]{:S(2)}) copy-start(bf16[128,256]{1,0:T(8,128)(2,1)} %param.32) | copy-start | bytes 196612
  97.9 22.5 %collective-permute-start.12 = (f32[2,128,128]{2,1,0:T(8,128)S(1)}, f32[2,128,128]{2,1,0:T(8,128)S(1)}, u32[]{:S(2)}, u32[]{:S(2)}) collective-permute-start(f32[2,128,128]{2,1,0:T(8,128)S(1)} %get-tuple-element.1863), channel_id=1, source_target_pairs={{0,16},{16,32},{32,48},{48,64},{64,80},{80,96},{96,112},{112,128},... | collective-permute-start | bytes 393224 | tf_op jit(solution)/shard_map/ppermute | solution.py:24
  100.0 13.9 %collective-permute-start.2 = (f32[2,128,128]{2,1,0:T(8,128)S(1)}, f32[2,128,128]{2,1,0:T(8,128)S(1)}, u32[]{:S(2)}, u32[]{:S(2)}) collective-permute-start(f32[2,128,128]{2,1,0:T(8,128)S(1)} %bitcast.783), channel_id=1, source_target_pairs={{16,0},{32,16},{48,32},{64,48},{80,64},{96,80},{112,96},{128,112},... | collective-permute-start | bytes 393224 | tf_op jit(solution)/shard_map/ppermute | solution.py:24
  102.4 13.2 %collective-permute-start.10 = (f32[2,128,128]{2,1,0:T(8,128)S(1)}, f32[2,128,128]{2,1,0:T(8,128)S(1)}, u32[]{:S(2)}, u32[]{:S(2)}) collective-permute-start(f32[2,128,128]{2,1,0:T(8,128)S(1)} %get-tuple-element.1864), channel_id=1, source_target_pairs={{0,16},{16,32},{32,48},{48,64},{64,80},{80,96},{96,112},{112,128},... | collective-permute-start | bytes 393224 | tf_op jit(solution)/shard_map/ppermute | solution.py:24
  105.7 21.9 %copy-start.9 = (s32[4096]{0:T(1024)}, s32[4096]{0:T(1024)S(1)}, u32[]{:S(2)}) copy-start(s32[4096]{0:T(1024)S(1)} %add_select_fusion) | copy-start | bytes 49156
  106.3 21.3 %copy-start.26 = (s32[128]{0:T(128)}, s32[128]{0:T(128)S(1)}, u32[]{:S(2)}) copy-start(s32[128]{0:T(128)S(1)} %get-tuple-element.2905) | copy-start | bytes 1540
  107.3 2.1 copy-start.22
  107.4 2.0 copy-start.14
  112.6 11.6 %collective-permute-start.1 = (f32[2,128,128]{2,1,0:T(8,128)S(1)}, f32[2,128,128]{2,1,0:T(8,128)S(1)}, u32[]{:S(2)}, u32[]{:S(2)}) collective-permute-start(f32[2,128,128]{2,1,0:T(8,128)S(1)} %fusion.278), channel_id=1, source_target_pairs={{32,0},{48,16},{64,32},{80,48},{96,64},{112,80},{128,96},{144,112}... | collective-permute-start | bytes 393224 | tf_op jit(solution)/shard_map/ppermute | solution.py:24
  114.3 11.5 %collective-permute-start.4 = (f32[2,128,128]{2,1,0:T(8,128)S(1)}, f32[2,128,128]{2,1,0:T(8,128)S(1)}, u32[]{:S(2)}, u32[]{:S(2)}) collective-permute-start(f32[2,128,128]{2,1,0:T(8,128)S(1)} %convolution_select_fusion.7), channel_id=1, source_target_pairs={{32,0},{48,16},{64,32},{80,48},{96,64},{112,80},{128,96},{144,112}... | collective-permute-start | bytes 393224 | tf_op jit(solution)/shard_map/ppermute | solution.py:24
  115.9 11.5 %collective-permute-start.11 = (f32[2,128,128]{2,1,0:T(8,128)S(1)}, f32[2,128,128]{2,1,0:T(8,128)S(1)}, u32[]{:S(2)}, u32[]{:S(2)}) collective-permute-start(f32[2,128,128]{2,1,0:T(8,128)S(1)} %fusion.273), channel_id=1, source_target_pairs={{0,32},{16,48},{32,64},{48,80},{64,96},{80,112},{96,128},{112,144}... | collective-permute-start | bytes 393224 | tf_op jit(solution)/shard_map/ppermute | solution.py:24
  120.8 13.0 %collective-permute-start.14 = (f32[2,128,128]{2,1,0:T(8,128)S(1)}, f32[2,128,128]{2,1,0:T(8,128)S(1)}, u32[]{:S(2)}, u32[]{:S(2)}) collective-permute-start(f32[2,128,128]{2,1,0:T(8,128)S(1)} %convolution_select_fusion.3), channel_id=1, source_target_pairs={{0,32},{16,48},{32,64},{48,80},{64,96},{80,112},{96,128},{112,144}... | collective-permute-start | bytes 393224 | tf_op jit(solution)/shard_map/ppermute | solution.py:24
  124.4 15.1 %collective-permute-start.3 = (f32[2,128,128]{2,1,0:T(8,128)S(1)}, f32[2,128,128]{2,1,0:T(8,128)S(1)}, u32[]{:S(2)}, u32[]{:S(2)}) collective-permute-start(f32[2,128,128]{2,1,0:T(8,128)S(1)} %fusion.277), channel_id=1, source_target_pairs={{64,0},{80,16},{96,32},{112,48},{128,64},{144,80},{160,96},{176,11... | collective-permute-start | bytes 393224 | tf_op jit(solution)/shard_map/ppermute | solution.py:24
  126.0 15.1 %collective-permute-start.6 = (f32[2,128,128]{2,1,0:T(8,128)S(1)}, f32[2,128,128]{2,1,0:T(8,128)S(1)}, u32[]{:S(2)}, u32[]{:S(2)}) collective-permute-start(f32[2,128,128]{2,1,0:T(8,128)S(1)} %convolution_select_fusion.6), channel_id=1, source_target_pairs={{64,0},{80,16},{96,32},{112,48},{128,64},{144,80},{160,96},{176,11... | collective-permute-start | bytes 393224 | tf_op jit(solution)/shard_map/ppermute | solution.py:24
  127.6 15.1 %collective-permute-start.13 = (f32[2,128,128]{2,1,0:T(8,128)S(1)}, f32[2,128,128]{2,1,0:T(8,128)S(1)}, u32[]{:S(2)}, u32[]{:S(2)}) collective-permute-start(f32[2,128,128]{2,1,0:T(8,128)S(1)} %fusion.272), channel_id=1, source_target_pairs={{0,64},{16,80},{32,96},{48,112},{64,128},{80,144},{96,160},{112,17... | collective-permute-start | bytes 393224 | tf_op jit(solution)/shard_map/ppermute | solution.py:24
  134.1 19.0 %collective-permute-start.16 = (f32[2,128,128]{2,1,0:T(8,128)S(1)}, f32[2,128,128]{2,1,0:T(8,128)S(1)}, u32[]{:S(2)}, u32[]{:S(2)}) collective-permute-start(f32[2,128,128]{2,1,0:T(8,128)S(1)} %convolution_select_fusion.2), channel_id=1, source_target_pairs={{0,64},{16,80},{32,96},{48,112},{64,128},{80,144},{96,160},{112,17... | collective-permute-start | bytes 393224 | tf_op jit(solution)/shard_map/ppermute | solution.py:24
  139.8 20.8 %collective-permute-start.5 = (f32[2,128,128]{2,1,0:T(8,128)S(1)}, f32[2,128,128]{2,1,0:T(8,128)S(1)}, u32[]{:S(2)}, u32[]{:S(2)}) collective-permute-start(f32[2,128,128]{2,1,0:T(8,128)S(1)} %fusion.276), channel_id=1, source_target_pairs={{128,0},{144,16},{160,32},{176,48},{192,64},{208,80},{224,96},{240... | collective-permute-start | bytes 393224 | tf_op jit(solution)/shard_map/ppermute | solution.py:24
  141.4 39.9 %collective-permute-start.8 = (f32[2,128,128]{2,1,0:T(8,128)S(1)}, f32[2,128,128]{2,1,0:T(8,128)S(1)}, u32[]{:S(2)}, u32[]{:S(2)}) collective-permute-start(f32[2,128,128]{2,1,0:T(8,128)S(1)} %convolution_select_fusion.5), channel_id=1, source_target_pairs={{128,0},{144,16},{160,32},{176,48},{192,64},{208,80},{224,96},{240... | collective-permute-start | bytes 393224 | tf_op jit(solution)/shard_map/ppermute | solution.py:24
  143.0 19.3 %collective-permute-start.15 = (f32[2,128,128]{2,1,0:T(8,128)S(1)}, f32[2,128,128]{2,1,0:T(8,128)S(1)}, u32[]{:S(2)}, u32[]{:S(2)}) collective-permute-start(f32[2,128,128]{2,1,0:T(8,128)S(1)} %fusion.271), channel_id=1, source_target_pairs={{0,128},{16,144},{32,160},{48,176},{64,192},{80,208},{96,224},{112... | collective-permute-start | bytes 393224 | tf_op jit(solution)/shard_map/ppermute | solution.py:24
  153.4 28.2 %collective-permute-start.18 = (f32[2,128,128]{2,1,0:T(8,128)S(1)}, f32[2,128,128]{2,1,0:T(8,128)S(1)}, u32[]{:S(2)}, u32[]{:S(2)}) collective-permute-start(f32[2,128,128]{2,1,0:T(8,128)S(1)} %convolution_select_fusion.1), channel_id=1, source_target_pairs={{0,128},{16,144},{32,160},{48,176},{64,192},{80,208},{96,224},{112... | collective-permute-start | bytes 393224 | tf_op jit(solution)/shard_map/ppermute | solution.py:24
  160.9 29.0 %collective-permute-start.7 = (f32[2,128,128]{2,1,0:T(8,128)S(1)}, f32[2,128,128]{2,1,0:T(8,128)S(1)}, u32[]{:S(2)}, u32[]{:S(2)}) collective-permute-start(f32[2,128,128]{2,1,0:T(8,128)S(1)} %fusion.275), channel_id=1, source_target_pairs={{256,0},{272,16},{288,32},{304,48},{320,64},{336,80},{352,96},{368... | collective-permute-start | bytes 393224 | tf_op jit(solution)/shard_map/ppermute | solution.py:24
  162.5 20.5 %collective-permute-start.17 = (f32[2,128,128]{2,1,0:T(8,128)S(1)}, f32[2,128,128]{2,1,0:T(8,128)S(1)}, u32[]{:S(2)}, u32[]{:S(2)}) collective-permute-start(f32[2,128,128]{2,1,0:T(8,128)S(1)} %fusion.270), channel_id=1, source_target_pairs={{0,256},{16,272},{32,288},{48,304},{64,320},{80,336},{96,352},{112... | collective-permute-start | bytes 393224 | tf_op jit(solution)/shard_map/ppermute | solution.py:24
  183.3 11.6 %collective-permute-start.19 = (f32[2,128,128]{2,1,0:T(8,128)S(1)}, f32[2,128,128]{2,1,0:T(8,128)S(1)}, u32[]{:S(2)}, u32[]{:S(2)}) collective-permute-start(f32[2,128,128]{2,1,0:T(8,128)S(1)} %fusion.269), channel_id=1, source_target_pairs={{0,16},{16,32},{32,48},{48,64},{64,80},{80,96},{96,112},{112,128},... | collective-permute-start | bytes 393224 | tf_op jit(solution)/shard_map/ppermute | solution.py:24
  190.9 45.4 %collective-permute-start.9 = (f32[2,128,128]{2,1,0:T(8,128)}, f32[2,128,128]{2,1,0:T(8,128)S(1)}, u32[]{:S(2)}, u32[]{:S(2)}) collective-permute-start(f32[2,128,128]{2,1,0:T(8,128)} %fusion.274), channel_id=1, source_target_pairs={{16,0},{32,16},{48,32},{64,48},{80,64},{96,80},{112,96},{128,112},... | collective-permute-start | bytes 393224 | tf_op jit(solution)/shard_map/ppermute | solution.py:24
  253.6 14.6 %copy-start.6 = (f32[2,2,64]{2,1,0:T(2,128)S(1)}, f32[2,2,64]{2,1,0:T(2,128)}, u32[]{:S(2)}) copy-start(f32[2,2,64]{2,1,0:T(2,128)} %get-tuple-element.3932) | copy-start | bytes 3076 | tf_op jit(solution)/shard_map/transpose(jvp())/while
  287.0 14.6 %copy-start.6 = (f32[2,2,64]{2,1,0:T(2,128)S(1)}, f32[2,2,64]{2,1,0:T(2,128)}, u32[]{:S(2)}) copy-start(f32[2,2,64]{2,1,0:T(2,128)} %get-tuple-element.3932) | copy-start | bytes 3076 | tf_op jit(solution)/shard_map/transpose(jvp())/while
  318.1 3.9 copy-start.12
  318.1 6.7 %copy-start.10 = (s32[4096]{0:T(1024)S(1)}, s32[4096]{0:T(1024)}, u32[]{:S(2)}) copy-start(s32[4096]{0:T(1024)} %copy-done.9) | copy-start | bytes 49156
  318.1 6.7 %copy-start.27 = (s32[128]{0:T(128)S(1)}, s32[128]{0:T(128)}, u32[]{:S(2)}) copy-start(s32[128]{0:T(128)} %copy-done.26) | copy-start | bytes 1540
  318.1 6.7 %copy-start.30 = (f32[1,4096]{1,0:T(1,128)S(1)}, f32[1,4096]{1,0:T(1,128)}, u32[]{:S(2)}) copy-start(f32[1,4096]{1,0:T(1,128)} %param.33) | copy-start | bytes 49156
  318.1 6.7 %copy-start.32 = (s32[128]{0:T(128)S(1)}, s32[128]{0:T(128)}, u32[]{:S(2)}) copy-start(s32[128]{0:T(128)} %get-tuple-element.2906) | copy-start | bytes 1540
  324.8 6.1 %copy-start = (bf16[4096,1024]{1,0:T(8,128)(2,1)S(1)}, bf16[4096,1024]{1,0:T(8,128)(2,1)}, u32[]{:S(2)}) copy-start(bf16[4096,1024]{1,0:T(8,128)(2,1)} %all-gather.2.cloned.1.call-done) | copy-start | bytes 25165828
  327.8 3.1 copy-start.11
  333.1 1.8 copy-start.5
  (8 other events, 8.0 us)
Sparse Core Ops, SparseCore 0:
  11.3 85.5 all-gather.1
  334.1 124.0 all-reduce.4

commit v2 on v1

--- a/solution.py
+++ b/solution.py
@@ -24,7 +24,7 @@
     return jax.tree.map(lambda part: lax.ppermute(part, axis, pairs), value)
 
 
-def exclusive_scans(forward, backward, axis, join):
+def exclusive_scans(forward, backward, axis, join, hold):
     count, mine = (lax.axis_size(axis), lax.axis_index(axis))
     step = 1
     while step < count:
@@ -35,12 +35,25 @@
         else:
             got_f = shifted(forward, axis, step, False)
             got_b = shifted(backward, axis, step, True)
+        if step == 1:
+            got_f, got_b, hold = lax.optimization_barrier((got_f, got_b, hold))
         new_f = join(got_f, forward, last)
         new_b = join(got_b, backward, last)
         forward = jax.tree.map(lambda n, o: jnp.where(mine >= step, n, o), new_f, forward)
         backward = jax.tree.map(lambda n, o: jnp.where(mine + step < count, n, o), new_b, backward)
         step *= 2
-    return (shifted(forward[1], axis, 1, False), shifted(backward[1], axis, 1, True))
+    return (shifted(forward[1], axis, 1, False), shifted(backward[1], axis, 1, True), hold)
+
+
+def butterfly_sum(value, axis, start, stop):
+    count = lax.axis_size(axis)
+    dist = start
+    while dist < stop:
+        pairs = [(i, i ^ dist) for i in range(count)]
+        got = jax.tree.map(lambda part: lax.ppermute(part, axis, pairs), value)
+        value = jax.tree.map(jnp.add, value, got)
+        dist *= 2
+    return value
 
 
 def unit_rows(matrix):
@@ -261,10 +274,7 @@
         jnp.einsum("hnk,nhd->kd", dscores, queries.astype(jnp.float32), precision=HIGHEST)
         * score_scale
     )
-    slot_mask = (jnp.arange(KV_HEADS) == kv_group)[None, :, None]
-    key_slots = jnp.where(slot_mask, grad_key[:, None, :], 0.0).reshape(tok_rows, KV_HEADS * HD)
-    value_slots = jnp.where(slot_mask, grad_value[:, None, :], 0.0).reshape(tok_rows, KV_HEADS * HD)
-    attn_dk, attn_dv = lax.psum((key_slots, value_slots), "head")
+    group_devices = max(1, (Q_HEADS // KV_HEADS) // local_heads)
     raw_inputs = (
         gdn_q.astype(jnp.float32),
         gdn_k.astype(jnp.float32),
@@ -291,11 +301,24 @@
     written_end = outputs_zero[1]
     cot_full = gdn_cot.astype(jnp.float32)
     local_grad = pull_zero((cot_full, zero_memory))[1]
-    memory_in, memory_grad = exclusive_scans(
+    memory_in, memory_grad, (grad_q, group_sums) = exclusive_scans(
         (transition, written_end),
         (jnp.swapaxes(transition, 1, 2), local_grad),
         "ctx",
         compose_maps,
+        (grad_q, (grad_key, grad_value)),
+    )
+    group_sums = butterfly_sum(group_sums, "head", 1, group_devices)
+    slot_mask = (jnp.arange(KV_HEADS) == kv_group)[None, :, None]
+    key_slots = jnp.where(slot_mask, group_sums[0][:, None, :], 0.0).reshape(tok_rows, KV_HEADS * HD)
+    value_slots = jnp.where(slot_mask, group_sums[1][:, None, :], 0.0).reshape(
+        tok_rows, KV_HEADS * HD
+    )
+    attn_dk, attn_dv = butterfly_sum(
+        (key_slots, value_slots), "head", group_devices, lax.axis_size("head")
+    )
+    memory_in, memory_grad, grad_q, attn_dk, attn_dv = lax.optimization_barrier(
+        (memory_in, memory_grad, grad_q, attn_dk, attn_dv)
     )
     unused_out, pull_final = jax.vjp(local_run, raw_inputs, memory_in)
     grads = pull_final((cot_full, memory_grad))[0]

time: 471 us -> 352 us (0.75)
  waiting for transfers between devices: 128 us -> 24.1 us
  local copies, waits for them, and re-layouts: 47.7 us -> 30.6 us
  starting transfers between devices: 87 us -> 91.8 us
    psum x1 -> x0, waiting for transfers between devices: 122 us -> none  [on_device(): attn_dk, attn_dv = lax.psum((key_slots, value_slots), 'head')]
    ppermute x0 -> x8, starting transfers between devices: none -> 24.1 us  [butterfly_sum(): got = jax.tree.map(lambda part: lax.ppermute(part, axis, pairs), value)]
    ppermute x20, starting transfers between devices: 86.9 us -> 67.7 us  [shifted(): return jax.tree.map(lambda part: lax.ppermute(part, axis, pairs), value)]
    ppermute x20, waiting for transfers between devices: 5.92 us -> 24 us  [shifted(): return jax.tree.map(lambda part: lax.ppermute(part, axis, pairs), value)]
    another operation x31, local copies, waits for them, and re-layouts: 6.17 us -> 1.38 us
  transfers between devices with their start and end apart: 22 -> 29, of which waited for: 3 -> 3; matrix products, arithmetic and copies ran while one was open for 46% -> 31% of each run, Pallas kernels for 0% -> 0%
where the time goes in v2:
time: 352 us; the launch traced here: 350 us
  other arithmetic  144 us (41%)
  starting transfers between devices  91.8 us (26%)
  matrix products  42.5 us (12%)
  local copies, waits for them, and re-layouts  30.6 us (9%)
  waiting for transfers between devices  24.1 us (7%)
  between operations  15.7 us (4%)
    another operation x44, other arithmetic, span_update(): lax.linalg.triangular_solve(system, target, left_side=True, lower=True, u...  119 us
    ppermute x20, starting transfers between devices, shifted(): return jax.tree.map(lambda part: lax.ppermute(part, axis, pairs), value)  67.7 us
    ppermute x8, starting transfers between devices, butterfly_sum(): got = jax.tree.map(lambda part: lax.ppermute(part, axis, pairs), value)  24.1 us
    ppermute x20, waiting for transfers between devices, shifted(): return jax.tree.map(lambda part: lax.ppermute(part, axis, pairs), value)  24 us
  transfers between devices with their start and end apart: 29, of which 3 were waited for; matrix products, arithmetic and copies ran while one was open for 31% of the time, Pallas kernels for 0%

profile of v2, /device:TPU:1, one launch (start us, length us, event | category | flops | bytes accessed | tf_op | source)
XLA Modules:
  0.0 350.1 jit_solution(1648471126465347261)
XLA Ops:
  9.5 1.6 pad_maximum_fusion
  12.7 23.7 %while.143 = (s32[]{:T(128)}, f32[2,128,128]{2,1,0:T(8,128)S(1)}, f32[2,2,64]{2,1,0:T(2,128)S(1)}, f32[2,2,64]{2,1,0:T(2,128)S(1)}, f32[2,2,64,128]{3,2,1,0:T(8,128)S(1)}, /*index=5*/s32[]{:T(128)}, f32[]{:T(128)}) while((s32[]{:T(128)}, f32[2,128,128]{2,1,0:T(8,128)S(1)}, f32[2,2,64]{2,1,0:T(2,128)S(1)}, f32[2,2,64]{2,1,0:T(2,128)S(1)}, ...), condition=%wide.region_3.5_spmd, body=%wide.region_1.4_spmd.sunk | while | flops 75726912 | bytes 1051793 | solution.py:116
  13.9 9.8 %custom-call.41 = f32[2,1,64,64]{2,3,1,0:T(8,128)S(1)} custom-call(f32[2,1,64,64]{3,2,1,0:T(8,128)S(1)} %fusion.467), custom_call_target="InvertDiagBlocksLowerTriangular" | custom-call | tf_op jit(solution)/shard_map/while/body/eval_jaxpr/triangular_solve/custom-call.1 | solution.py:78
  25.8 9.8 %custom-call.41 = f32[2,1,64,64]{2,3,1,0:T(8,128)S(1)} custom-call(f32[2,1,64,64]{3,2,1,0:T(8,128)S(1)} %fusion.467), custom_call_target="InvertDiagBlocksLowerTriangular" | custom-call | tf_op jit(solution)/shard_map/while/body/eval_jaxpr/triangular_solve/custom-call.1 | solution.py:78
  36.4 4.9 %collective-permute-start = (f32[2,128,128]{2,1,0:T(8,128)S(1)}, f32[2,128,128]{2,1,0:T(8,128)}, u32[]{:S(2)}, u32[]{:S(2)}) collective-permute-start(f32[2,128,128]{2,1,0:T(8,128)S(1)} %get-tuple-element.1868), channel_id=1, source_target_pairs={{0,16},{16,32},{32,48},{48,64},{64,80},{80,96},{96,112},{112,128},... | collective-permute-start | bytes 393224 | tf_op jit(solution)/shard_map/ppermute | solution.py:24
  42.7 24.4 %while.147 = (s32[]{:T(128)}, f32[2,128,128]{2,1,0:T(8,128)S(1)}, f32[2,2,64,1]{2,1,3,0:T(2,128)S(1)}, f32[2,2,64,1]{2,1,3,0:T(2,128)S(1)}, f32[2,2,64,64]{3,2,1...) while((s32[]{:T(128)}, f32[2,128,128]{2,1,0:T(8,128)S(1)}, ...), condition=%wide.region_7.9_spmd.clone.clone, body=%wide.region_5.8_spmd.clone.clone.sunk | while | flops 88404160 | bytes 1474303 | solution.py:116
  44.0 9.8 %custom-call.46 = f32[2,1,64,64]{2,3,1,0:T(8,128)S(1)} custom-call(f32[2,1,64,64]{3,2,1,0:T(8,128)S(1)} %add_bitcast_fusion.8), custom_call_target="InvertDiagBlocksLowerTriangular" | custom-call | tf_op jit(solution)/shard_map/jvp()/while/body/eval_jaxpr/triangular_solve/custom-call.1 | solution.py:78
  56.2 9.8 %custom-call.46 = f32[2,1,64,64]{2,3,1,0:T(8,128)S(1)} custom-call(f32[2,1,64,64]{3,2,1,0:T(8,128)S(1)} %add_bitcast_fusion.8), custom_call_target="InvertDiagBlocksLowerTriangular" | custom-call | tf_op jit(solution)/shard_map/jvp()/while/body/eval_jaxpr/triangular_solve/custom-call.1 | solution.py:78
  67.1 1.9 collective-permute-start.1
  69.8 5.7 %collective-permute-start.2 = (f32[2,128,128]{2,1,0:T(8,128)}, f32[2,128,128]{2,1,0:T(8,128)}, u32[]{:S(2)}, u32[]{:S(2)}) collective-permute-start(f32[2,128,128]{2,1,0:T(8,128)} %bitcast.10), channel_id=1, source_target_pairs={{16,0},{32,16},{48,32},{64,48},{80,64},{96,80},{112,96},{128,112},... | collective-permute-start | bytes 393224 | tf_op jit(solution)/shard_map/ppermute | solution.py:24
  75.7 23.6 %while.146 = (s32[]{:T(128)}, f32[2,128,128]{2,1,0:T(8,128)S(1)}, f32[2,2,1,1]{1,3,2,0:T(1,128)S(1)}, f32[2,2,64,1]{2,1,3,0:T(2,128)S(1)}, f32[2,2,64,128]{3,2,1...) while((s32[]{:T(128)}, f32[2,128,128]{2,1,0:T(8,128)S(1)}, ...), condition=%wide.region_9.12_spmd.clone, body=%wide.region_8.11_spmd.clone.sunk | while | flops 100954176 | bytes 1590979 | solution.py:116
  77.0 9.8 %custom-call.45 = f32[2,1,64,64]{2,3,1,0:T(8,128)S(1)} custom-call(f32[2,1,64,64]{3,2,1,0:T(8,128)S(1)} %fusion.532), custom_call_target="InvertDiagBlocksLowerTriangular" | custom-call | tf_op jit(solution)/shard_map/transpose(jvp())/while/body/eval_jaxpr/triangular_solve/custom-call.0 | solution.py:78
  88.8 9.8 %custom-call.45 = f32[2,1,64,64]{2,3,1,0:T(8,128)S(1)} custom-call(f32[2,1,64,64]{3,2,1,0:T(8,128)S(1)} %fusion.532), custom_call_target="InvertDiagBlocksLowerTriangular" | custom-call | tf_op jit(solution)/shard_map/transpose(jvp())/while/body/eval_jaxpr/triangular_solve/custom-call.0 | solution.py:78
  99.3 2.1 collective-permute-start.3
  108.6 3.9 %fusion.306 = (bf16[4096,256]{1,0:T(8,128)(2,1)S(1)}, bf16[4096,256]{1,0:T(8,128)(2,1)}) fusion(bf16[4096,1024]{1,0:T(8,128)(2,1)} %all-gather.2.cloned.1.call-done), kind=kLoop, calls=%fused_computation.511 | loop fusion | bytes 8388608 | tf_op jit(solution)/shard_map/slice | solution.py:229
  112.5 2.3 gather_fusion
  114.8 1.4 gather_fusion.1
  117.3 1.3 fusion.264
  119.1 3.3 fusion.249
  130.4 2.5 collective-permute-start.6
  135.4 1.4 convolution_select_fusion.7
  138.1 3.2 collective-permute-start.24
  141.3 2.1 collective-permute-start.20
  143.7 8.3 %collective-permute-start.5 = (f32[2,128,128]{2,1,0:T(8,128)S(1)}, f32[2,128,128]{2,1,0:T(8,128)S(1)}, u32[]{:S(2)}, u32[]{:S(2)}) collective-permute-start(f32[2,128,128]{2,1,0:T(8,128)S(1)} %fusion.277), channel_id=1, source_target_pairs={{0,64},{16,80},{32,96},{48,112},{64,128},{80,144},{96,160},{112,17... | collective-permute-start | bytes 393224 | tf_op jit(solution)/shard_map/ppermute | solution.py:24
  152.3 5.7 %collective-permute-start.8 = (f32[2,128,128]{2,1,0:T(8,128)S(1)}, f32[2,128,128]{2,1,0:T(8,128)S(1)}, u32[]{:S(2)}, u32[]{:S(2)}) collective-permute-start(f32[2,128,128]{2,1,0:T(8,128)S(1)} %convolution_select_fusion.5), channel_id=1, source_target_pairs={{0,64},{16,80},{32,96},{48,112},{64,128},{80,144},{96,160},{112,17... | collective-permute-start | bytes 393224 | tf_op jit(solution)/shard_map/ppermute | solution.py:24
  161.2 4.8 %collective-permute-start.25 = (f32[128,256]{1,0:T(8,128)S(1)}, f32[128,256]{1,0:T(8,128)S(1)}, u32[]{:S(2)}, u32[]{:S(2)}) collective-permute-start(f32[128,256]{1,0:T(8,128)S(1)} %add.378), channel_id=1, source_target_pairs={{0,2},{1,3},{2,0},{3,1},{4,6},{5,7},{6,4},{7,5},{8,10},{9,11},{10,... | collective-permute-start | bytes 393224 | tf_op jit(solution)/shard_map/ppermute | solution.py:53
  166.1 2.0 collective-permute-start.21
  168.4 10.1 %collective-permute-start.7 = (f32[2,128,128]{2,1,0:T(8,128)S(1)}, f32[2,128,128]{2,1,0:T(8,128)S(1)}, u32[]{:S(2)}, u32[]{:S(2)}) collective-permute-start(f32[2,128,128]{2,1,0:T(8,128)S(1)} %fusion.276), channel_id=1, source_target_pairs={{0,128},{16,144},{32,160},{48,176},{64,192},{80,208},{96,224},{112... | collective-permute-start | bytes 393224 | tf_op jit(solution)/shard_map/ppermute | solution.py:24
  178.7 7.5 %collective-permute-start.10 = (f32[2,128,128]{2,1,0:T(8,128)S(1)}, f32[2,128,128]{2,1,0:T(8,128)S(1)}, u32[]{:S(2)}, u32[]{:S(2)}) collective-permute-start(f32[2,128,128]{2,1,0:T(8,128)S(1)} %convolution_select_fusion.4), channel_id=1, source_target_pairs={{0,128},{16,144},{32,160},{48,176},{64,192},{80,208},{96,224},{112... | collective-permute-start | bytes 393224 | tf_op jit(solution)/shard_map/ppermute | solution.py:24
  189.5 3.1 collective-permute-start.26
  192.7 2.2 collective-permute-start.22
  195.1 20.4 %collective-permute-done.15 = f32[2,128,128]{2,1,0:T(8,128)S(1)} collective-permute-done((f32[2,128,128]{2,1,0:T(8,128)S(1)}, f32[2,128,128]{2,1,0:T(8,128)S(1)}, u32[]{:S(2)}, u32[]{:S(2)}) %collective-permute-start.15) | collective-permute-done | bytes 131104 | tf_op jit(solution)/shard_map/ppermute | solution.py:24
  215.5 2.4 collective-permute-start.9
  219.9 4.6 %collective-permute-start.23 = (f32[128,512]{1,0:T(8,128)S(1)}, f32[128,512]{1,0:T(8,128)S(1)}, u32[]{:S(2)}, u32[]{:S(2)}) collective-permute-start(f32[128,512]{1,0:T(8,128)S(1)} %get-tuple-element.2922), channel_id=1, source_target_pairs={{0,8},{1,9},{2,10},{3,11},{4,12},{5,13},{6,14},{7,15},{8,0},{9,1},... | collective-permute-start | bytes 786440 | tf_op jit(solution)/shard_map/ppermute | solution.py:53
  224.5 2.1 collective-permute-start.27
  227.5 1.9 collective-permute-start.11
  229.5 3.1 collective-permute-done.17
  232.9 4.3 %collective-permute-start.19 = (f32[2,128,128]{2,1,0:T(8,128)S(1)}, f32[2,128,128]{2,1,0:T(8,128)S(1)}, u32[]{:S(2)}, u32[]{:S(2)}) collective-permute-start(f32[2,128,128]{2,1,0:T(8,128)S(1)} %fusion.269), channel_id=1, source_target_pairs={{16,0},{32,16},{48,32},{64,48},{80,64},{96,80},{112,96},{128,112},... | collective-permute-start | bytes 393224 | tf_op jit(solution)/shard_map/ppermute | solution.py:24
  239.5 28.3 %while.144 = (s32[]{:T(128)}, f32[2,128,128]{2,1,0:T(8,128)S(1)}, f32[2,2,64,64]{3,2,1,0:T(8,128)S(1)}, f32[2,2,64,64]{3,2,1,0:T(8,128)S(1)}, f32[2,2,64,64]{3,2...) while((s32[]{:T(128)}, f32[2,128,128]{2,1,0:T(8,128)S(1)}, ...), condition=%wide.region_14.17_spmd.clone.clone, body=%wide.region_12.16_spmd.clone.clone.sunk | while | flops 113643840 | bytes 2896277 | solution.py:116
  241.3 9.8 %custom-call.42 = f32[2,1,64,64]{2,3,1,0:T(8,128)S(1)} custom-call(f32[2,1,64,64]{3,2,1,0:T(8,128)S(1)} %add_bitcast_fusion.6), custom_call_target="InvertDiagBlocksLowerTriangular" | custom-call | tf_op jit(solution)/shard_map/jvp()/while/body/eval_jaxpr/triangular_solve/custom-call.1 | solution.py:78
  255.4 9.8 %custom-call.42 = f32[2,1,64,64]{2,3,1,0:T(8,128)S(1)} custom-call(f32[2,1,64,64]{3,2,1,0:T(8,128)S(1)} %add_bitcast_fusion.6), custom_call_target="InvertDiagBlocksLowerTriangular" | custom-call | tf_op jit(solution)/shard_map/jvp()/while/body/eval_jaxpr/triangular_solve/custom-call.1 | solution.py:78
  269.6 63.0 %while.145 = (s32[]{:T(128)}, f32[2,128,128]{2,1,0:T(8,128)S(1)}, f32[2,2,64,128]{3,2,1,0:T(8,128)S(1)}, f32[2,2,64,128]{3,2,1,0:T(8,128)S(1)}, f32[2,2,64,128]{...) while((s32[]{:T(128)}, f32[2,128,128]{2,1,0:T(8,128)S(1)}, ...), condition=%wide.region_26.29_spmd.clone.clone, body=%wide.region_15.28_spmd.clone.clone.sunk | while | flops 258757312 | bytes 5321257 | solution.py:116
  273.9 9.8 %custom-call.43 = f32[2,1,64,64]{2,3,1,0:T(8,128)S(1)} custom-call(f32[2,1,64,64]{3,2,1,0:T(8,128)S(1)} %fusion.506), custom_call_target="InvertDiagBlocksLowerTriangular" | custom-call | tf_op jit(solution)/shard_map/transpose(jvp())/while/body/eval_jaxpr/triangular_solve/custom-call.0 | solution.py:78
  286.0 9.8 %custom-call.44 = f32[2,1,64,64]{2,3,1,0:T(8,128)S(1)} custom-call(f32[2,1,64,64]{3,2,1,0:T(8,128)S(1)} %add_bitcast_fusion.7), custom_call_target="InvertDiagBlocksLowerTriangular" | custom-call | tf_op jit(solution)/shard_map/transpose(jvp())/while/body/eval_jaxpr/triangular_solve | solution.py:78
  305.4 9.8 %custom-call.43 = f32[2,1,64,64]{2,3,1,0:T(8,128)S(1)} custom-call(f32[2,1,64,64]{3,2,1,0:T(8,128)S(1)} %fusion.506), custom_call_target="InvertDiagBlocksLowerTriangular" | custom-call | tf_op jit(solution)/shard_map/transpose(jvp())/while/body/eval_jaxpr/triangular_solve/custom-call.0 | solution.py:78
  317.6 9.8 %custom-call.44 = f32[2,1,64,64]{2,3,1,0:T(8,128)S(1)} custom-call(f32[2,1,64,64]{3,2,1,0:T(8,128)S(1)} %add_bitcast_fusion.7), custom_call_target="InvertDiagBlocksLowerTriangular" | custom-call | tf_op jit(solution)/shard_map/transpose(jvp())/while/body/eval_jaxpr/triangular_solve | solution.py:78
  334.1 1.4 add_add_fusion.1
  337.0 1.3 add_add_fusion
  (461 shorter events, 92.5 us)
Async XLA Ops:
  7.2 101.4 %all-gather.2.cloned.1.call-start = ((), (), s32[]{:S(2)}) async-start(), calls=%async_computation | async-start | bytes 8650752 | tf_op jit(solution)/shard_map/all_gather | solution.py:227
  12.3 29.0 %copy-start.17 = (bf16[128,256]{1,0:T(8,128)(2,1)S(1)}, bf16[128,256]{1,0:T(8,128)(2,1)}, u32[]{:S(2)}) copy-start(bf16[128,256]{1,0:T(8,128)(2,1)} %param.38) | copy-start | bytes 196612
  12.3 29.1 %copy-start.6 = (bf16[128,128]{1,0:T(8,128)(2,1)S(1)}, bf16[128,128]{1,0:T(8,128)(2,1)}, u32[]{:S(2)}) copy-start(bf16[128,128]{1,0:T(8,128)(2,1)} %param.36) | copy-start | bytes 98308
  36.4 90.3 %collective-permute-start = (f32[2,128,128]{2,1,0:T(8,128)S(1)}, f32[2,128,128]{2,1,0:T(8,128)}, u32[]{:S(2)}, u32[]{:S(2)}) collective-permute-start(f32[2,128,128]{2,1,0:T(8,128)S(1)} %get-tuple-element.1868), channel_id=1, source_target_pairs={{0,16},{16,32},{32,48},{48,64},{64,80},{80,96},{96,112},{112,128},... | collective-permute-start | bytes 393224 | tf_op jit(solution)/shard_map/ppermute | solution.py:24
  42.3 33.3 %copy-start.18 = (bf16[128,256]{1,0:T(8,128)(2,1)S(1)}, bf16[128,256]{1,0:T(8,128)(2,1)}, u32[]{:S(2)}) copy-start(bf16[128,256]{1,0:T(8,128)(2,1)} %param.43) | copy-start | bytes 196612
  67.1 8.4 %copy-start.15 = (f32[2,2,64]{2,1,0:T(2,128)}, f32[2,2,64]{2,1,0:T(2,128)S(1)}, u32[]{:S(2)}) copy-start(f32[2,2,64]{2,1,0:T(2,128)S(1)} %get-tuple-element.4018) | copy-start | bytes 3076
  67.1 8.5 %copy-start.11 = (f32[2,2,64]{2,1,0:T(2,128)}, f32[2,2,64]{2,1,0:T(2,128)S(1)}, u32[]{:S(2)}) copy-start(f32[2,2,64]{2,1,0:T(2,128)S(1)} %get-tuple-element.4014) | copy-start | bytes 3076
  67.1 59.6 %collective-permute-start.1 = (f32[2,128,128]{2,1,0:T(8,128)S(1)}, f32[2,128,128]{2,1,0:T(8,128)}, u32[]{:S(2)}, u32[]{:S(2)}) collective-permute-start(f32[2,128,128]{2,1,0:T(8,128)S(1)} %get-tuple-element.1869), channel_id=1, source_target_pairs={{0,16},{16,32},{32,48},{48,64},{64,80},{80,96},{96,112},{112,128},... | collective-permute-start | bytes 393224 | tf_op jit(solution)/shard_map/ppermute | solution.py:24
  69.8 56.9 %collective-permute-start.2 = (f32[2,128,128]{2,1,0:T(8,128)}, f32[2,128,128]{2,1,0:T(8,128)}, u32[]{:S(2)}, u32[]{:S(2)}) collective-permute-start(f32[2,128,128]{2,1,0:T(8,128)} %bitcast.10), channel_id=1, source_target_pairs={{16,0},{32,16},{48,32},{64,48},{80,64},{96,80},{112,96},{128,112},... | collective-permute-start | bytes 393224 | tf_op jit(solution)/shard_map/ppermute | solution.py:24
  75.7 25.9 %copy-start.25 = (s32[1,64,4]{1,2,0:T(4,128)S(1)}, s32[1,64,4]{1,2,0:T(4,128)}, u32[]{:S(2)}) copy-start(s32[1,64,4]{1,2,0:T(4,128)} %param.35) | copy-start | bytes 3076
  75.7 31.9 %copy-start.13 = (bf16[128,256]{1,0:T(8,128)(2,1)S(1)}, bf16[128,256]{1,0:T(8,128)(2,1)}, u32[]{:S(2)}) copy-start(bf16[128,256]{1,0:T(8,128)(2,1)} %param.29) | copy-start | bytes 196612
  75.7 32.1 %copy-start.5 = (bf16[128,256]{1,0:T(8,128)(2,1)S(1)}, bf16[128,256]{1,0:T(8,128)(2,1)}, u32[]{:S(2)}) copy-start(bf16[128,256]{1,0:T(8,128)(2,1)} %param.32) | copy-start | bytes 196612
  99.3 27.4 %collective-permute-start.3 = (f32[2,128,128]{2,1,0:T(8,128)S(1)}, f32[2,128,128]{2,1,0:T(8,128)}, u32[]{:S(2)}, u32[]{:S(2)}) collective-permute-start(f32[2,128,128]{2,1,0:T(8,128)S(1)} %get-tuple-element.1876), channel_id=1, source_target_pairs={{16,0},{32,16},{48,32},{64,48},{80,64},{96,80},{112,96},{128,112},... | collective-permute-start | bytes 393224 | tf_op jit(solution)/shard_map/ppermute | solution.py:24
  101.4 11.0 %copy-start.3 = (bf16[128,1,256]{2,0,1:T(8,128)(2,1)}, bf16[128,1,256]{2,0,1:T(8,128)(2,1)S(1)}, u32[]{:S(2)}) copy-start(bf16[128,1,256]{2,0,1:T(8,128)(2,1)S(1)} %copy.139) | copy-start | bytes 196612
  101.6 10.9 %copy-start.1 = (bf16[128,1,256]{2,0,1:T(8,128)(2,1)}, bf16[128,1,256]{2,0,1:T(8,128)(2,1)S(1)}, u32[]{:S(2)}) copy-start(bf16[128,1,256]{2,0,1:T(8,128)(2,1)S(1)} %copy.140) | copy-start | bytes 196612
  102.7 5.9 %copy-start.33 = (f32[2,64]{1,0:T(2,128)}, f32[2,64]{1,0:T(2,128)S(1)}, u32[]{:S(2)}) copy-start(f32[2,64]{1,0:T(2,128)S(1)} %sub.346) | copy-start | bytes 1540
  102.7 5.8 %copy-start.26 = (f32[2,64]{1,0:T(2,128)}, f32[2,64]{1,0:T(2,128)S(1)}, u32[]{:S(2)}) copy-start(f32[2,64]{1,0:T(2,128)S(1)} %sub.349) | copy-start | bytes 1540
  117.3 5.1 %copy-start = (bf16[4096,1024]{1,0:T(8,128)(2,1)S(1)}, bf16[4096,1024]{1,0:T(8,128)(2,1)}, u32[]{:S(2)}) copy-start(bf16[4096,1024]{1,0:T(8,128)(2,1)} %all-gather.2.cloned.1.call-done) | copy-start | bytes 25165828
  127.9 13.4 %collective-permute-start.4 = (f32[2,128,128]{2,1,0:T(8,128)S(1)}, f32[2,128,128]{2,1,0:T(8,128)S(1)}, u32[]{:S(2)}, u32[]{:S(2)}) collective-permute-start(f32[2,128,128]{2,1,0:T(8,128)S(1)} %fusion.278), channel_id=1, source_target_pairs={{0,32},{16,48},{32,64},{48,80},{64,96},{80,112},{96,128},{112,144}... | collective-permute-start | bytes 393224 | tf_op jit(solution)/shard_map/ppermute | solution.py:24
  130.4 13.3 %collective-permute-start.6 = (f32[2,128,128]{2,1,0:T(8,128)S(1)}, f32[2,128,128]{2,1,0:T(8,128)S(1)}, u32[]{:S(2)}, u32[]{:S(2)}) collective-permute-start(f32[2,128,128]{2,1,0:T(8,128)S(1)} %convolution_select_fusion.6), channel_id=1, source_target_pairs={{0,32},{16,48},{32,64},{48,80},{64,96},{80,112},{96,128},{112,144}... | collective-permute-start | bytes 393224 | tf_op jit(solution)/shard_map/ppermute | solution.py:24
  134.1 18.1 %collective-permute-start.12 = (f32[2,128,128]{2,1,0:T(8,128)S(1)}, f32[2,128,128]{2,1,0:T(8,128)S(1)}, u32[]{:S(2)}, u32[]{:S(2)}) collective-permute-start(f32[2,128,128]{2,1,0:T(8,128)S(1)} %fusion.273), channel_id=1, source_target_pairs={{32,0},{48,16},{64,32},{80,48},{96,64},{112,80},{128,96},{144,112}... | collective-permute-start | bytes 393224 | tf_op jit(solution)/shard_map/ppermute | solution.py:24
  136.8 21.5 %collective-permute-start.14 = (f32[2,128,128]{2,1,0:T(8,128)S(1)}, f32[2,128,128]{2,1,0:T(8,128)S(1)}, u32[]{:S(2)}, u32[]{:S(2)}) collective-permute-start(f32[2,128,128]{2,1,0:T(8,128)S(1)} %convolution_select_fusion.7), channel_id=1, source_target_pairs={{32,0},{48,16},{64,32},{80,48},{96,64},{112,80},{128,96},{144,112}... | collective-permute-start | bytes 393224 | tf_op jit(solution)/shard_map/ppermute | solution.py:24
  138.1 21.8 %collective-permute-start.24 = (f32[128,256]{1,0:T(8,128)S(1)}, f32[128,256]{1,0:T(8,128)S(1)}, u32[]{:S(2)}, u32[]{:S(2)}) collective-permute-start(f32[128,256]{1,0:T(8,128)S(1)} %fusion.254), channel_id=1, source_target_pairs={{0,1},{1,0},{2,3},{3,2},{4,5},{5,4},{6,7},{7,6},{8,9},{9,8},{10,11... | collective-permute-start | bytes 393224 | tf_op jit(solution)/shard_map/ppermute | solution.py:53
  141.3 19.9 %collective-permute-start.20 = (f32[128,256]{1,0:T(8,128)S(1)}, f32[128,256]{1,0:T(8,128)S(1)}, u32[]{:S(2)}, u32[]{:S(2)}) collective-permute-start(f32[128,256]{1,0:T(8,128)S(1)} %fusion.279), channel_id=1, source_target_pairs={{0,1},{1,0},{2,3},{3,2},{4,5},{5,4},{6,7},{7,6},{8,9},{9,8},{10,11... | collective-permute-start | bytes 393224 | tf_op jit(solution)/shard_map/ppermute | solution.py:53
  143.7 22.4 %collective-permute-start.5 = (f32[2,128,128]{2,1,0:T(8,128)S(1)}, f32[2,128,128]{2,1,0:T(8,128)S(1)}, u32[]{:S(2)}, u32[]{:S(2)}) collective-permute-start(f32[2,128,128]{2,1,0:T(8,128)S(1)} %fusion.277), channel_id=1, source_target_pairs={{0,64},{16,80},{32,96},{48,112},{64,128},{80,144},{96,160},{112,17... | collective-permute-start | bytes 393224 | tf_op jit(solution)/shard_map/ppermute | solution.py:24
  152.3 16.1 %collective-permute-start.8 = (f32[2,128,128]{2,1,0:T(8,128)S(1)}, f32[2,128,128]{2,1,0:T(8,128)S(1)}, u32[]{:S(2)}, u32[]{:S(2)}) collective-permute-start(f32[2,128,128]{2,1,0:T(8,128)S(1)} %convolution_select_fusion.5), channel_id=1, source_target_pairs={{0,64},{16,80},{32,96},{48,112},{64,128},{80,144},{96,160},{112,17... | collective-permute-start | bytes 393224 | tf_op jit(solution)/shard_map/ppermute | solution.py:24
  158.3 20.4 %collective-permute-start.13 = (f32[2,128,128]{2,1,0:T(8,128)S(1)}, f32[2,128,128]{2,1,0:T(8,128)S(1)}, u32[]{:S(2)}, u32[]{:S(2)}) collective-permute-start(f32[2,128,128]{2,1,0:T(8,128)S(1)} %fusion.272), channel_id=1, source_target_pairs={{64,0},{80,16},{96,32},{112,48},{128,64},{144,80},{160,96},{176,11... | collective-permute-start | bytes 393224 | tf_op jit(solution)/shard_map/ppermute | solution.py:24
  159.9 26.7 %collective-permute-start.16 = (f32[2,128,128]{2,1,0:T(8,128)S(1)}, f32[2,128,128]{2,1,0:T(8,128)S(1)}, u32[]{:S(2)}, u32[]{:S(2)}) collective-permute-start(f32[2,128,128]{2,1,0:T(8,128)S(1)} %convolution_select_fusion.2), channel_id=1, source_target_pairs={{64,0},{80,16},{96,32},{112,48},{128,64},{144,80},{160,96},{176,11... | collective-permute-start | bytes 393224 | tf_op jit(solution)/shard_map/ppermute | solution.py:24
  161.2 26.9 %collective-permute-start.25 = (f32[128,256]{1,0:T(8,128)S(1)}, f32[128,256]{1,0:T(8,128)S(1)}, u32[]{:S(2)}, u32[]{:S(2)}) collective-permute-start(f32[128,256]{1,0:T(8,128)S(1)} %add.378), channel_id=1, source_target_pairs={{0,2},{1,3},{2,0},{3,1},{4,6},{5,7},{6,4},{7,5},{8,10},{9,11},{10,... | collective-permute-start | bytes 393224 | tf_op jit(solution)/shard_map/ppermute | solution.py:53
  166.1 23.4 %collective-permute-start.21 = (f32[128,256]{1,0:T(8,128)S(1)}, f32[128,256]{1,0:T(8,128)S(1)}, u32[]{:S(2)}, u32[]{:S(2)}) collective-permute-start(f32[128,256]{1,0:T(8,128)S(1)} %add.374), channel_id=1, source_target_pairs={{0,2},{1,3},{2,0},{3,1},{4,6},{5,7},{6,4},{7,5},{8,10},{9,11},{10,... | collective-permute-start | bytes 393224 | tf_op jit(solution)/shard_map/ppermute | solution.py:53
  168.4 24.3 %collective-permute-start.7 = (f32[2,128,128]{2,1,0:T(8,128)S(1)}, f32[2,128,128]{2,1,0:T(8,128)S(1)}, u32[]{:S(2)}, u32[]{:S(2)}) collective-permute-start(f32[2,128,128]{2,1,0:T(8,128)S(1)} %fusion.276), channel_id=1, source_target_pairs={{0,128},{16,144},{32,160},{48,176},{64,192},{80,208},{96,224},{112... | collective-permute-start | bytes 393224 | tf_op jit(solution)/shard_map/ppermute | solution.py:24
  178.7 45.8 %collective-permute-start.10 = (f32[2,128,128]{2,1,0:T(8,128)S(1)}, f32[2,128,128]{2,1,0:T(8,128)S(1)}, u32[]{:S(2)}, u32[]{:S(2)}) collective-permute-start(f32[2,128,128]{2,1,0:T(8,128)S(1)} %convolution_select_fusion.4), channel_id=1, source_target_pairs={{0,128},{16,144},{32,160},{48,176},{64,192},{80,208},{96,224},{112... | collective-permute-start | bytes 393224 | tf_op jit(solution)/shard_map/ppermute | solution.py:24
  186.6 29.0 %collective-permute-start.15 = (f32[2,128,128]{2,1,0:T(8,128)S(1)}, f32[2,128,128]{2,1,0:T(8,128)S(1)}, u32[]{:S(2)}, u32[]{:S(2)}) collective-permute-start(f32[2,128,128]{2,1,0:T(8,128)S(1)} %fusion.271), channel_id=1, source_target_pairs={{128,0},{144,16},{160,32},{176,48},{192,64},{208,80},{224,96},{240... | collective-permute-start | bytes 393224 | tf_op jit(solution)/shard_map/ppermute | solution.py:24
  188.2 38.8 %collective-permute-start.18 = (f32[2,128,128]{2,1,0:T(8,128)S(1)}, f32[2,128,128]{2,1,0:T(8,128)S(1)}, u32[]{:S(2)}, u32[]{:S(2)}) collective-permute-start(f32[2,128,128]{2,1,0:T(8,128)S(1)} %convolution_select_fusion.1), channel_id=1, source_target_pairs={{128,0},{144,16},{160,32},{176,48},{192,64},{208,80},{224,96},{240... | collective-permute-start | bytes 393224 | tf_op jit(solution)/shard_map/ppermute | solution.py:24
  189.5 30.3 %copy-start.36 = (pred[512]{0:T(512)(128)(4,1)S(1)}, pred[512]{0:T(512)(128)(4,1)}, u32[]{:S(2)}) copy-start(pred[512]{0:T(512)(128)(4,1)} %broadcast_in_dim.489) | copy-start | bytes 1540
  189.5 28.7 %collective-permute-start.26 = (f32[128,256]{1,0:T(8,128)S(1)}, f32[128,256]{1,0:T(8,128)S(1)}, u32[]{:S(2)}, u32[]{:S(2)}) collective-permute-start(f32[128,256]{1,0:T(8,128)S(1)} %add.379), channel_id=1, source_target_pairs={{0,4},{1,5},{2,6},{3,7},{4,0},{5,1},{6,2},{7,3},{8,12},{9,13},{10,... | collective-permute-start | bytes 393224 | tf_op jit(solution)/shard_map/ppermute | solution.py:53
  192.7 27.0 %collective-permute-start.22 = (f32[128,256]{1,0:T(8,128)S(1)}, f32[128,256]{1,0:T(8,128)S(1)}, u32[]{:S(2)}, u32[]{:S(2)}) collective-permute-start(f32[128,256]{1,0:T(8,128)S(1)} %add.375), channel_id=1, source_target_pairs={{0,4},{1,5},{2,6},{3,7},{4,0},{5,1},{6,2},{7,3},{8,12},{9,13},{10,... | collective-permute-start | bytes 393224 | tf_op jit(solution)/shard_map/ppermute | solution.py:53
  215.5 11.7 %collective-permute-start.9 = (f32[2,128,128]{2,1,0:T(8,128)S(1)}, f32[2,128,128]{2,1,0:T(8,128)S(1)}, u32[]{:S(2)}, u32[]{:S(2)}) collective-permute-start(f32[2,128,128]{2,1,0:T(8,128)S(1)} %fusion.275), channel_id=1, source_target_pairs={{0,256},{16,272},{32,288},{48,304},{64,320},{80,336},{96,352},{112... | collective-permute-start | bytes 393224 | tf_op jit(solution)/shard_map/ppermute | solution.py:24
  218.2 14.4 %collective-permute-start.17 = (f32[2,128,128]{2,1,0:T(8,128)S(1)}, f32[2,128,128]{2,1,0:T(8,128)S(1)}, u32[]{:S(2)}, u32[]{:S(2)}) collective-permute-start(f32[2,128,128]{2,1,0:T(8,128)S(1)} %fusion.270), channel_id=1, source_target_pairs={{256,0},{272,16},{288,32},{304,48},{320,64},{336,80},{352,96},{368... | collective-permute-start | bytes 393224 | tf_op jit(solution)/shard_map/ppermute | solution.py:24
  219.6 17.5 %copy-start.39 = (s32[64]{0:T(128)S(1)}, s32[64]{0:T(128)}, u32[]{:S(2)}) copy-start(s32[64]{0:T(128)} %iota_add_fusion.5) | copy-start | bytes 772
  219.9 17.4 %collective-permute-start.23 = (f32[128,512]{1,0:T(8,128)S(1)}, f32[128,512]{1,0:T(8,128)S(1)}, u32[]{:S(2)}, u32[]{:S(2)}) collective-permute-start(f32[128,512]{1,0:T(8,128)S(1)} %get-tuple-element.2922), channel_id=1, source_target_pairs={{0,8},{1,9},{2,10},{3,11},{4,12},{5,13},{6,14},{7,15},{8,0},{9,1},... | collective-permute-start | bytes 786440 | tf_op jit(solution)/shard_map/ppermute | solution.py:53
  224.5 13.4 %collective-permute-start.27 = (f32[128,512]{1,0:T(8,128)S(1)}, f32[128,512]{1,0:T(8,128)S(1)}, u32[]{:S(2)}, u32[]{:S(2)}) collective-permute-start(f32[128,512]{1,0:T(8,128)S(1)} %get-tuple-element.2921), channel_id=1, source_target_pairs={{0,8},{1,9},{2,10},{3,11},{4,12},{5,13},{6,14},{7,15},{8,0},{9,1},... | collective-permute-start | bytes 786440 | tf_op jit(solution)/shard_map/ppermute | solution.py:53
  227.5 12.0 %copy-start.12 = (f32[2,2,64]{2,1,0:T(2,128)S(1)}, f32[2,2,64]{2,1,0:T(2,128)}, u32[]{:S(2)}) copy-start(f32[2,2,64]{2,1,0:T(2,128)} %copy-done.11) | copy-start | bytes 3076
  227.5 12.0 %copy-start.16 = (f32[2,2,64]{2,1,0:T(2,128)S(1)}, f32[2,2,64]{2,1,0:T(2,128)}, u32[]{:S(2)}) copy-start(f32[2,2,64]{2,1,0:T(2,128)} %copy-done.15) | copy-start | bytes 3076
  227.5 11.2 %collective-permute-start.11 = (f32[2,128,128]{2,1,0:T(8,128)S(1)}, f32[2,128,128]{2,1,0:T(8,128)S(1)}, u32[]{:S(2)}, u32[]{:S(2)}) collective-permute-start(f32[2,128,128]{2,1,0:T(8,128)S(1)} %fusion.274), channel_id=1, source_target_pairs={{0,16},{16,32},{32,48},{48,64},{64,80},{80,96},{96,112},{112,128},... | collective-permute-start | bytes 393224 | tf_op jit(solution)/shard_map/ppermute | solution.py:24
  232.9 6.3 %collective-permute-start.19 = (f32[2,128,128]{2,1,0:T(8,128)S(1)}, f32[2,128,128]{2,1,0:T(8,128)S(1)}, u32[]{:S(2)}, u32[]{:S(2)}) collective-permute-start(f32[2,128,128]{2,1,0:T(8,128)S(1)} %fusion.269), channel_id=1, source_target_pairs={{16,0},{32,16},{48,32},{64,48},{80,64},{96,80},{112,96},{128,112},... | collective-permute-start | bytes 393224 | tf_op jit(solution)/shard_map/ppermute | solution.py:24
  269.6 63.0 %copy-start.7 = (bf16[128,128]{1,0:T(8,128)(2,1)S(1)}, bf16[128,128]{1,0:T(8,128)(2,1)}, u32[]{:S(2)}) copy-start(bf16[128,128]{1,0:T(8,128)(2,1)} %param.36) | copy-start | bytes 98308
  269.6 65.9 %copy-start.9 = (bf16[128,128]{1,0:T(8,128)(2,1)S(1)}, bf16[128,128]{1,0:T(8,128)(2,1)}, u32[]{:S(2)}) copy-start(bf16[128,128]{1,0:T(8,128)(2,1)} %param.37) | copy-start | bytes 98308
  (25 other events, 55.7 us)
Sparse Core Ops, SparseCore 0:
  11.3 86.9 all-gather.1
